TPU v7x, 256 devices: a whole 4x4x8 slice. The times are simulated.
256 devices in a mesh: neuron: 32 (over y, z), tm: 2 (over core), trial: 4 (over x).
Axes of the slice: x: 4, y: 4, z: 8, core: 2. Of those that a mesh axis runs over, the one named last changes fastest.
Arguments:
- tensor: bfloat16 [8192, 256, 512], P('neuron', 'tm', 'trial'), may hold values from -6 to 6
- present_blocks: int32 [64, 16], P('neuron'), may hold values 0 or 1
- trial_day: int32 [512], P('trial'), may hold values from 0 to 15
- time_factor: bfloat16 [256, 256], P('tm'), may hold values from 0 to 1
- trial_factor: bfloat16 [512, 256], P('trial'), may hold values from 0 to 1
Outputs:
- neuron_out: bfloat16 [8192, 256], P(('neuron', 'tm', 'trial'))
- time_out: bfloat16 [256, 256], P('tm')
- trial_out: bfloat16 [512, 256], P('trial')
All inputs are finite; a program needn't handle non-finite values. No bound on the sum of `present_blocks` on one device may be relied on, other than what follows from the above.
Results may differ from a plain program's by a relative error of at most 0.0051.
The roundings to bfloat16 on the way count: a program that leaves them out, or rounds other values in their place, can miss the bound.
Values may be sent and summed in bfloat16 or wider, within the bound.
No kernel may reach another device: no remote copies, remote signals or barrier semaphores. Data moves between devices by JAX's collectives and lax.ppermute only.
A program may use at most 128 MiB of HBM per device.

v0:
```python
import jax
import jax.numpy as jnp
from jax import lax
from jax.sharding import PartitionSpec as P

RIDGE = 0.1
EPSILON = 1e-06


def normal_inverse(gram_matrix):
    order_size = gram_matrix.shape[0]
    identity = jnp.eye(order_size, dtype=jnp.float32)
    scaled = gram_matrix / jnp.mean(jnp.diagonal(gram_matrix)) + RIDGE * identity
    lower_factor = jnp.linalg.cholesky(scaled)
    return jax.scipy.linalg.cho_solve((lower_factor, True), identity)


def apply_inverse(partial_sums, inverse):
    return jnp.dot(partial_sums, inverse, precision=lax.Precision.HIGHEST)


def raw_gram(raw_rows):
    return jnp.dot(raw_rows.T, raw_rows, precision=lax.Precision.HIGHEST)


def khatri_rao(left_rows, right_rows):
    return (
        left_rows.astype(jnp.float32)[:, None, :] * right_rows.astype(jnp.float32)[None, :, :]
    ).astype(jnp.bfloat16)


def rescale(raw_rows, gram_sum, total_rows):
    scales = jnp.sqrt(jnp.diagonal(gram_sum) / total_rows + EPSILON)
    factor = (raw_rows / scales[None, :]).astype(jnp.bfloat16)
    normed = gram_sum / (scales[:, None] * scales[None, :])
    return (factor, normed)


def mask_tensor(tensor, present_blocks, trial_day):
    day_count = present_blocks.shape[1]
    onehot = (trial_day[:, None] == jnp.arange(day_count, dtype=jnp.int32)[None, :]).astype(
        jnp.float32
    )
    block_mask = jnp.dot(present_blocks.astype(jnp.float32), onehot.T)
    block_count = present_blocks.shape[0]
    shaped = tensor.reshape(
        block_count, tensor.shape[0] // block_count, tensor.shape[1], tensor.shape[2]
    )
    return shaped * block_mask.astype(jnp.bfloat16)[:, None, None, :]


def on_device(tensor, present_blocks, trial_day, time_factor, trial_factor):
    blocks = mask_tensor(tensor, present_blocks, trial_day)
    block_count, block_rows, time_rows, trial_rows = blocks.shape
    neuron_rows = block_count * block_rows
    flattened = blocks.reshape(neuron_rows, time_rows, trial_rows)
    rank_size = time_factor.shape[1]
    start_time = lax.psum(
        jnp.dot(time_factor.T, time_factor, preferred_element_type=jnp.float32), "tm"
    )
    start_trial = lax.psum(
        jnp.dot(trial_factor.T, trial_factor, preferred_element_type=jnp.float32), "trial"
    )
    inverse_neuron = normal_inverse(start_time * start_trial)
    kr_tk = khatri_rao(time_factor, trial_factor)
    neuron_total = neuron_rows * lax.axis_size("neuron")
    tensor_piece = flattened
    partial_sums = lax.psum_scatter(
        jnp.einsum("itk,tkr->ir", tensor_piece, kr_tk, preferred_element_type=jnp.float32),
        ("tm", "trial"),
        scatter_dimension=0,
        tiled=True,
    )
    raw_rows = apply_inverse(partial_sums, inverse_neuron)
    gram_sum = lax.psum(raw_gram(raw_rows), ("neuron", "tm", "trial"))
    neuron_own, gram_neuron = rescale(raw_rows, gram_sum, neuron_total)
    neuron_local = lax.all_gather(neuron_own, ("tm", "trial"), axis=0, tiled=True)
    neuron_blocks = neuron_local.reshape(block_count, block_rows, rank_size)
    time_total = time_rows * lax.axis_size("tm")
    inverse_time = normal_inverse(gram_neuron * start_trial)
    own_time = time_rows // (lax.axis_size("neuron") * lax.axis_size("trial"))

    def time_add_block(running, inputs):
        tensor_piece, rows_a = inputs
        kr_ik = khatri_rao(rows_a, trial_factor)
        return (
            running
            + jnp.einsum("itk,ikr->tr", tensor_piece, kr_ik, preferred_element_type=jnp.float32),
            None,
        )

    running, unused = lax.scan(
        time_add_block,
        jnp.zeros((own_time * lax.axis_size(("neuron", "trial")), rank_size), jnp.float32),
        (blocks, neuron_blocks),
    )
    partial_sums = lax.psum_scatter(running, ("neuron", "trial"), scatter_dimension=0, tiled=True)
    raw_rows = apply_inverse(partial_sums, inverse_time)
    gram_sum = lax.psum(raw_gram(raw_rows), ("neuron", "tm", "trial"))
    time_own, gram_time = rescale(raw_rows, gram_sum, time_total)
    time_local = lax.all_gather(time_own, ("neuron", "trial"), axis=0, tiled=True)
    trial_total = trial_rows * lax.axis_size("trial")
    inverse_trial = normal_inverse(gram_neuron * gram_time)
    own_trial = trial_rows // (lax.axis_size("neuron") * lax.axis_size("tm"))

    def trial_add_block(running, inputs):
        tensor_piece, rows_a = inputs
        kr_it = khatri_rao(rows_a, time_local)
        return (
            running
            + jnp.einsum("itk,itr->kr", tensor_piece, kr_it, preferred_element_type=jnp.float32),
            None,
        )

    running, unused = lax.scan(
        trial_add_block,
        jnp.zeros((own_trial * lax.axis_size(("neuron", "tm")), rank_size), jnp.float32),
        (blocks, neuron_blocks),
    )
    partial_sums = lax.psum_scatter(running, ("neuron", "tm"), scatter_dimension=0, tiled=True)
    raw_rows = apply_inverse(partial_sums, inverse_trial)
    squares = lax.psum(jnp.sum(raw_rows * raw_rows, axis=0), ("neuron", "tm", "trial"))
    scales = jnp.sqrt(squares / trial_total + EPSILON)
    trial_own = (raw_rows / scales[None, :]).astype(jnp.bfloat16)
    trial_local = lax.all_gather(trial_own, ("neuron", "tm"), axis=0, tiled=True)
    return (neuron_own, time_local, trial_local)


def solution(mesh):
    return jax.shard_map(
        on_device,
        mesh=mesh,
        in_specs=(
            P("neuron", "tm", "trial"),
            P("neuron", None),
            P("trial"),
            P("tm", None),
            P("trial", None),
        ),
        out_specs=(P(("neuron", "tm", "trial"), None), P("tm", None), P("trial", None)),
        check_vma=False,
    )
```

profile of v0, /device:TPU:1, one launch (start us, length us, event | category | flops | bytes accessed | tf_op | source)
XLA Modules:
  0.0 1565.0 jit_solution(4462833593146219689)
XLA Ops:
  21.7 10.2 fusion.28
  32.2 11.3 copy.42
  43.5 16.4 %all-reduce.12.cloned.1.call-done = f32[256,256]{0,1:T(8,128)} async-done(((f32[256,256]{0,1:T(8,128)}), f32[256,256]{0,1:T(8,128)}) %all-reduce.12.cloned.1.call-update) | async-done | bytes 262160 | tf_op jit(solution)/shard_map/psum | solution.py:61
  59.9 34.9 %all-reduce.10.cloned.1.call-done = f32[256,256]{0,1:T(8,128)} async-done(((f32[256,256]{0,1:T(8,128)}), f32[256,256]{0,1:T(8,128)}) %all-reduce.10.cloned.1.call-update) | async-done | bytes 262160 | tf_op jit(solution)/shard_map/psum | solution.py:58
  99.7 11.7 cholesky.172
  111.5 9.8 custom-call.29
  121.8 11.7 cholesky.189
  139.3 19.9 %custom-call.30 = f32[2,128,128]{1,2,0:T(8,128)S(1)} custom-call(f32[2,128,128]{2,1,0:T(8,128)S(1)} %get-tuple-element.117), custom_call_target="InvertDiagBlocksLowerTriangular" | custom-call | tf_op jit(solution)/shard_map/jit(_cho_solve)/triangular_solve | solution.py:15
  171.2 245.8 %all-reduce.14.cloned.1.call-done = f32[256,256]{0,1:T(8,128)} async-done(((f32[256,256]{0,1:T(8,128)}), f32[256,256]{0,1:T(8,128)}) %all-reduce.14.cloned.1.call-update) | async-done | bytes 262160 | tf_op jit(solution)/shard_map/psum | solution.py:75
  419.6 23.8 %all_gather.9 = bf16[256,256]{1,0:T(8,128)(2,1)S(1)} all-gather(bf16[32,256]{1,0:T(8,128)(2,1)S(1)} %divide_convert_fusion), channel_id=1, replica_groups=mesh['neuron'=32,'tm'=2,'trial'=4] {'tm','trial'}, dimensions={0}, use_global_device_ids=true | all-gather | bytes 147456 | tf_op jit(solution)/shard_map/all_gather | solution.py:77
  456.0 11.7 cholesky.206
  467.8 9.8 custom-call.31
  478.1 11.7 cholesky.223
  496.2 19.8 %custom-call.32 = f32[2,128,128]{1,2,0:T(8,128)S(1)} custom-call(f32[2,128,128]{2,1,0:T(8,128)S(1)} %get-tuple-element.118), custom_call_target="InvertDiagBlocksLowerTriangular" | custom-call | tf_op jit(solution)/shard_map/jit(_cho_solve)/triangular_solve | solution.py:15
  518.0 142.0 %all-reduce.18.cloned.1.call-done = f32[128,256]{1,0:T(8,128)} async-done(((f32[128,256]{1,0:T(8,128)}), f32[128,256]{1,0:T(8,128)}) %all-reduce.18.cloned.1.call-update) | async-done | bytes 131088
  663.7 253.5 %all-reduce.16.cloned.1.call-done = f32[256,256]{0,1:T(8,128)} async-done(((f32[256,256]{0,1:T(8,128)}), f32[256,256]{0,1:T(8,128)}) %all-reduce.16.cloned.1.call-update) | async-done | bytes 262160 | tf_op jit(solution)/shard_map/psum | solution.py:99
  919.9 290.8 %all-gather.1 = bf16[128,1,256]{2,1,0:T(2,128)(2,1)S(1)} all-gather(bf16[1,1,256]{2,1,0:T(2,128)(2,1)S(1)} %reshape.150), channel_id=2, replica_groups=mesh['neuron'=32,'tm'=2,'trial'=4] {'neuron','trial'}, dimensions={0}, use_global_device_ids=true | all-gather | bytes 66048 | tf_op jit(solution)/shard_map/all_gather | solution.py:101
  1222.9 11.7 cholesky.240
  1234.6 9.8 custom-call.33
  1244.9 11.7 cholesky.257
  1263.4 19.9 %custom-call.34 = f32[2,128,128]{1,2,0:T(8,128)S(1)} custom-call(f32[2,128,128]{2,1,0:T(8,128)S(1)} %get-tuple-element.119), custom_call_target="InvertDiagBlocksLowerTriangular" | custom-call | tf_op jit(solution)/shard_map/jit(_cho_solve)/triangular_solve | solution.py:15
  1285.2 152.9 %all-reduce.20.cloned.1.call-done = f32[128,256]{1,0:T(8,128)} async-done(((f32[128,256]{1,0:T(8,128)}), f32[128,256]{1,0:T(8,128)}) %all-reduce.20.cloned.1.call-update) | async-done | bytes 131088
  1439.1 74.5 %psum.39 = f32[256]{0:T(256)S(1)} all-reduce(f32[256]{0:T(256)S(1)} %get-tuple-element.210), channel_id=1, replica_groups=mesh['neuron'=32,'tm'=2,'trial'=4] {'neuron','tm','trial'}, use_global_device_ids=true, to_apply=%region_19.22 | all-reduce | flops 256 | bytes 2048 | tf_op jit(solution)/shard_map/psum | solution.py:122
  1513.6 43.1 %all-gather.2 = bf16[64,2,256]{2,1,0:T(2,128)(2,1)S(1)} all-gather(bf16[1,2,256]{2,1,0:T(2,128)(2,1)S(1)} %fusion.82), channel_id=1, replica_groups=mesh['neuron'=32,'tm'=2,'trial'=4] {'neuron','tm'}, dimensions={0}, use_global_device_ids=true | all-gather | bytes 66560 | tf_op jit(solution)/shard_map/all_gather | solution.py:125
  (166 shorter events, 109.7 us)
Async XLA Ops:
  8.0 51.9 %all-reduce.12.cloned.1.call-start = ((), (), s32[]{:S(2)}) async-start(), calls=%async_computation.3 | async-start | bytes 524288 | tf_op jit(solution)/shard_map/psum | solution.py:61
  9.9 84.9 %all-reduce.10.cloned.1.call-start = ((), (), s32[]{:S(2)}) async-start(), calls=%async_computation.2 | async-start | bytes 524288 | tf_op jit(solution)/shard_map/psum | solution.py:58
  11.8 149.3 %reduce-scatter.2.cloned.1.call-start = ((), (), s32[]{:S(2)}) async-start(), calls=%async_computation.1 | async-start | bytes 294912 | tf_op jit(solution)/shard_map/reduce_scatter | solution.py:68
  31.9 385.1 %all-reduce.14.cloned.1.call-start = ((), (), s32[]{:S(2)}) async-start(), calls=%async_computation.4 | async-start | bytes 524288 | tf_op jit(solution)/shard_map/psum | solution.py:75
  163.3 496.8 %all-reduce.18.cloned.1.call-start = ((), (), s32[]{:S(2)}) async-start(), calls=%async_computation.6 | async-start | bytes 262144
  163.3 7.3 copy-start.9
  163.3 280.1 %copy-start.2 = (bf16[128,256]{1,0:T(8,128)(2,1)S(1)}, bf16[128,256]{1,0:T(8,128)(2,1)}, u32[]{:S(2)}) copy-start(bf16[128,256]{1,0:T(8,128)(2,1)} %param.16) | copy-start | bytes 196612
  419.6 23.8 %copy-start.7 = (bf16[32,256]{1,0:T(8,128)(2,1)}, bf16[32,256]{1,0:T(8,128)(2,1)S(1)}, u32[]{:S(2)}) copy-start(bf16[32,256]{1,0:T(8,128)(2,1)S(1)} %divide_convert_fusion) | copy-start | bytes 49156
  443.5 8.2 copy-start
  443.5 8.2 copy-start.4
  450.9 0.6 copy-start.6
  450.9 211.6 %copy-start.8 = (u32[256]{0:T(256)S(1)}, u32[256]{0:T(256)}, u32[]{:S(2)}) copy-start(u32[256]{0:T(256)} %constant.215) | copy-start | bytes 3076
  451.6 465.7 %all-reduce.16.cloned.1.call-start = ((), (), s32[]{:S(2)}) async-start(), calls=%async_computation.5 | async-start | bytes 524288 | tf_op jit(solution)/shard_map/psum | solution.py:99
  662.4 775.7 %all-reduce.20.cloned.1.call-start = ((), (), s32[]{:S(2)}) async-start(), calls=%async_computation.7 | async-start | bytes 262144
  1210.7 7.9 copy-start.1
  1217.9 0.7 copy-start.5
  1217.9 339.5 %copy-start.3 = (bf16[128,256]{1,0:T(8,128)(2,1)}, bf16[128,256]{1,0:T(8,128)(2,1)S(1)}, u32[]{:S(2)}) copy-start(bf16[128,256]{1,0:T(8,128)(2,1)S(1)} %get-tuple-element.461) | copy-start | bytes 196612
Sparse Core Ops, SparseCore 0:
  11.1 48.7 all-reduce.11
  62.5 32.2 all-reduce.9
  163.4 253.5 all-reduce.13
  662.5 254.6 all-reduce.15
Sparse Core Ops, SparseCore 1:
  32.0 38.7 reduce-scatter.1
  451.7 208.3 all-reduce.17
  1218.7 219.4 all-reduce.19
where the time goes:
time: 1570 us
  waiting for transfers between devices  846 us (54%)
  blocking collectives  432 us (28%)
  other arithmetic  184 us (12%)
  matrix products  40.6 us (3%)
  local copies, waits for them, and re-layouts  39.6 us (3%)
  between operations  22.6 us (1%)
    psum x2, waiting for transfers between devices, on_device(): gram_sum = lax.psum(raw_gram(raw_rows), ('neuron', 'tm', 'trial'))  499 us
    unnamed x9, waiting for transfers between devices  295 us
    all_gather x1, blocking collectives, on_device(): lax.all_gather(time_own, ('neuron', 'trial'), axis=0, tiled=True)  291 us
    another operation x20, other arithmetic, normal_inverse(): lower_factor = jnp.linalg.cholesky(scaled)  103 us
    psum x1, blocking collectives, on_device(): lax.psum(jnp.sum(raw_rows * raw_rows, axis=0), ('neuron', 'tm', 'trial'))  74.5 us
    another operation x7, other arithmetic, normal_inverse(): return jax.scipy.linalg.cho_solve((lower_factor, True), identity)  59.8 us
    all_gather x1, blocking collectives, on_device(): lax.all_gather(trial_own, ('neuron', 'tm'), axis=0, tiled=True)  43.1 us
    psum x1, waiting for transfers between devices, on_device(): lax.psum(jnp.dot(time_factor.T, time_factor, preferred_element_type=jnp.f...  34.9 us
  transfers between devices with their start and end apart: 7, of which 6 were waited for; matrix products, arithmetic and copies ran while one was open for 15% of the time, Pallas kernels for 0%

commit v1 on v0

--- a/solution.py
+++ b/solution.py
@@ -49,36 +49,36 @@
     return shaped * block_mask.astype(jnp.bfloat16)[:, None, None, :]
 
 
+def factor_gram(rows):
+    return jnp.dot(rows.T, rows, preferred_element_type=jnp.float32)
+
+
 def on_device(tensor, present_blocks, trial_day, time_factor, trial_factor):
+    time_all = lax.all_gather(time_factor, "tm", axis=0, tiled=True)
+    trial_all = lax.all_gather(trial_factor, "trial", axis=0, tiled=True)
     blocks = mask_tensor(tensor, present_blocks, trial_day)
     block_count, block_rows, time_rows, trial_rows = blocks.shape
     neuron_rows = block_count * block_rows
     flattened = blocks.reshape(neuron_rows, time_rows, trial_rows)
     rank_size = time_factor.shape[1]
-    start_time = lax.psum(
-        jnp.dot(time_factor.T, time_factor, preferred_element_type=jnp.float32), "tm"
-    )
-    start_trial = lax.psum(
-        jnp.dot(trial_factor.T, trial_factor, preferred_element_type=jnp.float32), "trial"
-    )
+    start_time = factor_gram(time_all)
+    start_trial = factor_gram(trial_all)
     inverse_neuron = normal_inverse(start_time * start_trial)
     kr_tk = khatri_rao(time_factor, trial_factor)
     neuron_total = neuron_rows * lax.axis_size("neuron")
-    tensor_piece = flattened
-    partial_sums = lax.psum_scatter(
-        jnp.einsum("itk,tkr->ir", tensor_piece, kr_tk, preferred_element_type=jnp.float32),
+    block_sums = lax.psum(
+        jnp.einsum("itk,tkr->ir", flattened, kr_tk, preferred_element_type=jnp.float32),
         ("tm", "trial"),
-        scatter_dimension=0,
-        tiled=True,
     )
-    raw_rows = apply_inverse(partial_sums, inverse_neuron)
-    gram_sum = lax.psum(raw_gram(raw_rows), ("neuron", "tm", "trial"))
-    neuron_own, gram_neuron = rescale(raw_rows, gram_sum, neuron_total)
-    neuron_local = lax.all_gather(neuron_own, ("tm", "trial"), axis=0, tiled=True)
+    raw_rows = apply_inverse(block_sums, inverse_neuron)
+    gram_sum = lax.psum(raw_gram(raw_rows), "neuron")
+    neuron_local, gram_neuron = rescale(raw_rows, gram_sum, neuron_total)
+    own_rows = neuron_rows // (lax.axis_size("tm") * lax.axis_size("trial"))
+    own_index = lax.axis_index("tm") * lax.axis_size("trial") + lax.axis_index("trial")
+    neuron_own = lax.dynamic_slice_in_dim(neuron_local, own_index * own_rows, own_rows, axis=0)
     neuron_blocks = neuron_local.reshape(block_count, block_rows, rank_size)
     time_total = time_rows * lax.axis_size("tm")
     inverse_time = normal_inverse(gram_neuron * start_trial)
-    own_time = time_rows // (lax.axis_size("neuron") * lax.axis_size("trial"))
 
     def time_add_block(running, inputs):
         tensor_piece, rows_a = inputs
@@ -91,17 +91,15 @@
 
     running, unused = lax.scan(
         time_add_block,
-        jnp.zeros((own_time * lax.axis_size(("neuron", "trial")), rank_size), jnp.float32),
+        jnp.zeros((time_rows, rank_size), jnp.float32),
         (blocks, neuron_blocks),
     )
-    partial_sums = lax.psum_scatter(running, ("neuron", "trial"), scatter_dimension=0, tiled=True)
-    raw_rows = apply_inverse(partial_sums, inverse_time)
-    gram_sum = lax.psum(raw_gram(raw_rows), ("neuron", "tm", "trial"))
-    time_own, gram_time = rescale(raw_rows, gram_sum, time_total)
-    time_local = lax.all_gather(time_own, ("neuron", "trial"), axis=0, tiled=True)
+    half_sums = lax.psum(running, ("neuron", "trial"))
+    raw_rows = apply_inverse(half_sums, inverse_time)
+    gram_sum = lax.psum(raw_gram(raw_rows), "tm")
+    time_local, gram_time = rescale(raw_rows, gram_sum, time_total)
     trial_total = trial_rows * lax.axis_size("trial")
     inverse_trial = normal_inverse(gram_neuron * gram_time)
-    own_trial = trial_rows // (lax.axis_size("neuron") * lax.axis_size("tm"))
 
     def trial_add_block(running, inputs):
         tensor_piece, rows_a = inputs
@@ -114,15 +112,14 @@
 
     running, unused = lax.scan(
         trial_add_block,
-        jnp.zeros((own_trial * lax.axis_size(("neuron", "tm")), rank_size), jnp.float32),
+        jnp.zeros((trial_rows, rank_size), jnp.float32),
         (blocks, neuron_blocks),
     )
-    partial_sums = lax.psum_scatter(running, ("neuron", "tm"), scatter_dimension=0, tiled=True)
-    raw_rows = apply_inverse(partial_sums, inverse_trial)
-    squares = lax.psum(jnp.sum(raw_rows * raw_rows, axis=0), ("neuron", "tm", "trial"))
+    quarter_sums = lax.psum(running, ("neuron", "tm"))
+    raw_rows = apply_inverse(quarter_sums, inverse_trial)
+    squares = lax.psum(jnp.sum(raw_rows * raw_rows, axis=0), "trial")
     scales = jnp.sqrt(squares / trial_total + EPSILON)
-    trial_own = (raw_rows / scales[None, :]).astype(jnp.bfloat16)
-    trial_local = lax.all_gather(trial_own, ("neuron", "tm"), axis=0, tiled=True)
+    trial_local = (raw_rows / scales[None, :]).astype(jnp.bfloat16)
     return (neuron_own, time_local, trial_local)
 
 

time: 1570 us -> 867 us (0.55)
  blocking collectives: 432 us -> 26.1 us
  waiting for transfers between devices: 846 us -> 554 us
    all_gather x3 -> x2, blocking collectives: 358 us -> 17.7 us  [the longest x1 11 us: on_device(): trial_all = lax.all_gather(trial_factor, 'trial', axis=0, tiled=True)]
    unnamed x9 -> x5, waiting for transfers between devices: 295 us -> 0.08 us
    psum x1, blocking collectives: 74.5 us -> 8.41 us  [on_device(): squares = lax.psum(jnp.sum(raw_rows * raw_rows, axis=0), 'trial')]
    psum x4 -> x5, waiting for transfers between devices: 551 us -> 554 us  [the longest x1 212 us: on_device(): half_sums = lax.psum(running, ('neuron', 'trial'))]
  transfers between devices with their start and end apart: 7 -> 5, of which waited for: 6 -> 4; matrix products, arithmetic and copies ran while one was open for 15% -> 10% of each run, Pallas kernels for 0% -> 0%
where the time goes in v1:
time: 867 us; the launch traced here: 863 us
  waiting for transfers between devices  554 us (64%)
  other arithmetic  184 us (21%)
  local copies, waits for them, and re-layouts  38.9 us (4%)
  matrix products  38.7 us (4%)
  blocking collectives  26.1 us (3%)
  between operations  20.2 us (2%)
    psum x1, waiting for transfers between devices, on_device(): half_sums = lax.psum(running, ('neuron', 'trial'))  212 us
    psum x1, waiting for transfers between devices, on_device(): quarter_sums = lax.psum(running, ('neuron', 'tm'))  177 us
    psum x1, waiting for transfers between devices, on_device(): gram_sum = lax.psum(raw_gram(raw_rows), 'neuron')  135 us
    another operation x20, other arithmetic, normal_inverse(): lower_factor = jnp.linalg.cholesky(scaled)  103 us
    another operation x7, other arithmetic, normal_inverse(): return jax.scipy.linalg.cho_solve((lower_factor, True), identity)  59.7 us
    psum x1, waiting for transfers between devices, on_device(): gram_sum = lax.psum(raw_gram(raw_rows), 'tm')  31 us
  transfers between devices with their start and end apart: 5, of which 4 were waited for; matrix products, arithmetic and copies ran while one was open for 10% of the time, Pallas kernels for 0%

profile of v1, /device:TPU:1, one launch (start us, length us, event | category | flops | bytes accessed | tf_op | source)
XLA Modules:
  0.0 862.6 jit_solution(6178857749009200221)
XLA Ops:
  9.9 7.2 broadcast_multiply_fusion.1
  17.1 9.9 %fusion.28 = f32[256,256]{1,0:T(8,128)} fusion(f32[128,256]{1,0:T(8,128)S(1)} %convert_element_type.81, f32[128,256]{1,0:T(8,128)S(1)} %convert_element_type.80, bf16[256,128,128]{2,1,0:T(8,128)(2,1)} %broadcast_multiply_fusion.1), kind=kOutput, calls=%fused_computation.39 | convolution fusion | flops 2155872256 | bytes 8912896 | tf_op jit(solution)/shard_map/itk,tkr->ir/dot_general | solution.py:70
  27.1 11.0 %all_gather.7 = bf16[512,256]{1,0:T(8,128)(2,1)S(1)} all-gather(bf16[128,256]{1,0:T(8,128)(2,1)S(1)} %copy-done.1), channel_id=1, replica_groups=mesh['neuron'=32,'tm'=2,'trial'=4] {'trial'}, dimensions={0}, use_global_device_ids=true | all-gather | bytes 327680 | tf_op jit(solution)/shard_map/all_gather | solution.py:58
  44.8 11.9 %copy.27 = bf16[256,128,128]{1,2,0:T(8,128)(2,1)} copy(bf16[256,128,128]{2,1,0:T(8,128)(2,1)} %param.12) | data formatting | bytes 16777216 | tf_op args[0]
  61.1 11.7 %cholesky.172 = f32[128,128]{1,0:T(8,128)S(1)} custom-call(f32[128,128]{1,0:T(8,128)S(1)} %cholesky.270), custom_call_target="Cholesky" | custom-call | tf_op jit(solution)/shard_map/jit(cholesky)/cholesky | solution.py:14
  72.8 9.8 %custom-call.29 = f32[1,128,128]{1,2,0:T(8,128)S(1)} custom-call(f32[1,128,128]{2,1,0:T(8,128)S(1)} %get-tuple-element.207), custom_call_target="InvertDiagBlocksLowerTriangular" | custom-call | tf_op jit(solution)/shard_map/jit(cholesky)/cholesky | solution.py:14
  83.2 11.7 %cholesky.189 = f32[128,128]{1,0:T(8,128)S(1)} custom-call(f32[128,128]{1,0:T(8,128)S(1)} %convolution_subtract_fusion.8), custom_call_target="Cholesky" | custom-call | tf_op jit(solution)/shard_map/jit(cholesky)/cholesky | solution.py:14
  101.0 19.8 %custom-call.30 = f32[2,128,128]{1,2,0:T(8,128)S(1)} custom-call(f32[2,128,128]{2,1,0:T(8,128)S(1)} %get-tuple-element.117), custom_call_target="InvertDiagBlocksLowerTriangular" | custom-call | tf_op jit(solution)/shard_map/jit(_cho_solve)/triangular_solve | solution.py:15
  125.5 7.2 broadcast_multiply_fusion
  132.8 134.7 %all-reduce.9.cloned.1.call-done = f32[256,256]{0,1:T(8,128)} async-done(((f32[256,256]{0,1:T(8,128)}), f32[256,256]{0,1:T(8,128)}) %all-reduce.9.cloned.1.call-update) | async-done | bytes 262160 | tf_op jit(solution)/shard_map/psum | solution.py:74
  275.1 11.7 %cholesky.206 = f32[128,128]{1,0:T(8,128)S(1)} custom-call(f32[128,128]{1,0:T(8,128)S(1)} %cholesky.273), custom_call_target="Cholesky" | custom-call | tf_op jit(solution)/shard_map/jit(cholesky)/cholesky | solution.py:14
  286.9 9.8 %custom-call.31 = f32[1,128,128]{1,2,0:T(8,128)S(1)} custom-call(f32[1,128,128]{2,1,0:T(8,128)S(1)} %get-tuple-element.203), custom_call_target="InvertDiagBlocksLowerTriangular" | custom-call | tf_op jit(solution)/shard_map/jit(cholesky)/cholesky | solution.py:14
  297.2 11.7 %cholesky.223 = f32[128,128]{1,0:T(8,128)S(1)} custom-call(f32[128,128]{1,0:T(8,128)S(1)} %convolution_subtract_fusion.7), custom_call_target="Cholesky" | custom-call | tf_op jit(solution)/shard_map/jit(cholesky)/cholesky | solution.py:14
  315.3 19.9 %custom-call.32 = f32[2,128,128]{1,2,0:T(8,128)S(1)} custom-call(f32[2,128,128]{2,1,0:T(8,128)S(1)} %get-tuple-element.118), custom_call_target="InvertDiagBlocksLowerTriangular" | custom-call | tf_op jit(solution)/shard_map/jit(_cho_solve)/triangular_solve | solution.py:15
  337.0 7.4 while.28
  345.3 211.6 %all-reduce.11.cloned.1.call-done = f32[128,256]{1,0:T(8,128)} async-done(((f32[128,256]{1,0:T(8,128)}), f32[128,256]{1,0:T(8,128)}) %all-reduce.11.cloned.1.call-update) | async-done | bytes 131088 | tf_op jit(solution)/shard_map/psum | solution.py:97
  560.1 31.0 %all-reduce.13.cloned.1.call-done = f32[256,256]{0,1:T(8,128)} async-done(((f32[256,256]{0,1:T(8,128)}), f32[256,256]{0,1:T(8,128)}) %all-reduce.13.cloned.1.call-update) | async-done | bytes 262160 | tf_op jit(solution)/shard_map/psum | solution.py:99
  599.1 11.7 %cholesky.240 = f32[128,128]{1,0:T(8,128)S(1)} custom-call(f32[128,128]{1,0:T(8,128)S(1)} %cholesky.276), custom_call_target="Cholesky" | custom-call | tf_op jit(solution)/shard_map/jit(cholesky)/cholesky | solution.py:14
  610.8 9.8 %custom-call.33 = f32[1,128,128]{1,2,0:T(8,128)S(1)} custom-call(f32[1,128,128]{2,1,0:T(8,128)S(1)} %get-tuple-element.199), custom_call_target="InvertDiagBlocksLowerTriangular" | custom-call | tf_op jit(solution)/shard_map/jit(cholesky)/cholesky | solution.py:14
  621.1 11.7 %cholesky.257 = f32[128,128]{1,0:T(8,128)S(1)} custom-call(f32[128,128]{1,0:T(8,128)S(1)} %convolution_subtract_fusion.6), custom_call_target="Cholesky" | custom-call | tf_op jit(solution)/shard_map/jit(cholesky)/cholesky | solution.py:14
  639.1 19.8 %custom-call.34 = f32[2,128,128]{1,2,0:T(8,128)S(1)} custom-call(f32[2,128,128]{2,1,0:T(8,128)S(1)} %get-tuple-element.119), custom_call_target="InvertDiagBlocksLowerTriangular" | custom-call | tf_op jit(solution)/shard_map/jit(_cho_solve)/triangular_solve | solution.py:15
  660.6 7.2 while.29
  668.8 176.8 %all-reduce.15.cloned.1.call-done = f32[128,256]{1,0:T(8,128)} async-done(((f32[128,256]{1,0:T(8,128)}), f32[128,256]{1,0:T(8,128)}) %all-reduce.15.cloned.1.call-update) | async-done | bytes 131088 | tf_op jit(solution)/shard_map/psum | solution.py:118
  846.8 8.4 psum.47
  (149 shorter events, 84.6 us)
Async XLA Ops:
  7.2 115.6 %all-reduce.7.cloned.1.call-start = ((), (), s32[]{:S(2)}) async-start(), calls=%async_computation | async-start | bytes 524288 | tf_op jit(solution)/shard_map/psum | solution.py:69
  17.0 10.0 %copy-start.1 = (bf16[128,256]{1,0:T(8,128)(2,1)S(1)}, bf16[128,256]{1,0:T(8,128)(2,1)}, u32[]{:S(2)}) copy-start(bf16[128,256]{1,0:T(8,128)(2,1)} %param.16) | copy-start | bytes 196612
  17.1 21.0 %copy-start.3 = (bf16[128,256]{1,0:T(8,128)(2,1)S(1)}, bf16[128,256]{1,0:T(8,128)(2,1)}, u32[]{:S(2)}) copy-start(bf16[128,256]{1,0:T(8,128)(2,1)} %param.15) | copy-start | bytes 196612
  27.0 240.5 %all-reduce.9.cloned.1.call-start = ((), (), s32[]{:S(2)}) async-start(), calls=%async_computation.1 | async-start | bytes 524288 | tf_op jit(solution)/shard_map/psum | solution.py:74
  125.4 431.5 %all-reduce.11.cloned.1.call-start = ((), (), s32[]{:S(2)}) async-start(), calls=%async_computation.2 | async-start | bytes 262144 | tf_op jit(solution)/shard_map/psum | solution.py:97
  336.9 256.8 %copy-start = (f32[256,256]{0,1:T(8,128)S(1)}, f32[256,256]{0,1:T(8,128)}, u32[]{:S(2)}) copy-start(f32[256,256]{0,1:T(8,128)} %all-reduce.9.cloned.1.call-done) | copy-start | bytes 786436
  344.3 0.6 copy-start.5
  345.0 246.1 %all-reduce.13.cloned.1.call-start = ((), (), s32[]{:S(2)}) async-start(), calls=%async_computation.3 | async-start | bytes 524288 | tf_op jit(solution)/shard_map/psum | solution.py:99
  559.3 286.3 %all-reduce.15.cloned.1.call-start = ((), (), s32[]{:S(2)}) async-start(), calls=%async_computation.4 | async-start | bytes 262144 | tf_op jit(solution)/shard_map/psum | solution.py:118
  667.8 0.7 copy-start.4
  667.8 188.1 %copy-start.2 = (bf16[128,256]{1,0:T(8,128)(2,1)}, bf16[128,256]{1,0:T(8,128)(2,1)S(1)}, u32[]{:S(2)}) copy-start(bf16[128,256]{1,0:T(8,128)(2,1)S(1)} %get-tuple-element.465) | copy-start | bytes 196612
Sparse Core Ops, SparseCore 0:
  27.1 67.2 all-reduce.6
  125.5 141.9 all-reduce.8
  345.1 211.7 all-reduce.10
  559.4 31.7 all-reduce.12
  668.6 176.9 all-reduce.14

commit v2 on v1

--- a/solution.py
+++ b/solution.py
@@ -49,36 +49,44 @@
     return shaped * block_mask.astype(jnp.bfloat16)[:, None, None, :]
 
 
+def tree_sum(values, axes):
+    for axis in axes:
+        size = lax.axis_size(axis)
+        stride = 1
+        while stride < size:
+            pairs = [(i, i ^ stride) for i in range(size)]
+            values = values + lax.ppermute(values, axis, pairs)
+            stride *= 2
+    return values
+
+
 def factor_gram(rows):
     return jnp.dot(rows.T, rows, preferred_element_type=jnp.float32)
 
 
 def on_device(tensor, present_blocks, trial_day, time_factor, trial_factor):
-    time_all = lax.all_gather(time_factor, "tm", axis=0, tiled=True)
-    trial_all = lax.all_gather(trial_factor, "trial", axis=0, tiled=True)
     blocks = mask_tensor(tensor, present_blocks, trial_day)
     block_count, block_rows, time_rows, trial_rows = blocks.shape
     neuron_rows = block_count * block_rows
     flattened = blocks.reshape(neuron_rows, time_rows, trial_rows)
     rank_size = time_factor.shape[1]
-    start_time = factor_gram(time_all)
-    start_trial = factor_gram(trial_all)
+    start_time = tree_sum(factor_gram(time_factor), ("tm",))
+    start_trial = tree_sum(factor_gram(trial_factor), ("trial",))
     inverse_neuron = normal_inverse(start_time * start_trial)
     kr_tk = khatri_rao(time_factor, trial_factor)
     neuron_total = neuron_rows * lax.axis_size("neuron")
-    block_sums = lax.psum(
+    block_sums = tree_sum(
         jnp.einsum("itk,tkr->ir", flattened, kr_tk, preferred_element_type=jnp.float32),
         ("tm", "trial"),
     )
     raw_rows = apply_inverse(block_sums, inverse_neuron)
-    gram_sum = lax.psum(raw_gram(raw_rows), "neuron")
+    gram_sum = tree_sum(raw_gram(raw_rows), ("neuron",))
     neuron_local, gram_neuron = rescale(raw_rows, gram_sum, neuron_total)
     own_rows = neuron_rows // (lax.axis_size("tm") * lax.axis_size("trial"))
     own_index = lax.axis_index("tm") * lax.axis_size("trial") + lax.axis_index("trial")
     neuron_own = lax.dynamic_slice_in_dim(neuron_local, own_index * own_rows, own_rows, axis=0)
     neuron_blocks = neuron_local.reshape(block_count, block_rows, rank_size)
     time_total = time_rows * lax.axis_size("tm")
-    inverse_time = normal_inverse(gram_neuron * start_trial)
 
     def time_add_block(running, inputs):
         tensor_piece, rows_a = inputs
@@ -94,12 +102,13 @@
         jnp.zeros((time_rows, rank_size), jnp.float32),
         (blocks, neuron_blocks),
     )
-    half_sums = lax.psum(running, ("neuron", "trial"))
+    running, gram_neuron = lax.optimization_barrier((running, gram_neuron))
+    half_sums = tree_sum(running, ("neuron", "trial"))
+    inverse_time = normal_inverse(gram_neuron * start_trial)
     raw_rows = apply_inverse(half_sums, inverse_time)
-    gram_sum = lax.psum(raw_gram(raw_rows), "tm")
+    gram_sum = tree_sum(raw_gram(raw_rows), ("tm",))
     time_local, gram_time = rescale(raw_rows, gram_sum, time_total)
     trial_total = trial_rows * lax.axis_size("trial")
-    inverse_trial = normal_inverse(gram_neuron * gram_time)
 
     def trial_add_block(running, inputs):
         tensor_piece, rows_a = inputs
@@ -115,9 +124,11 @@
         jnp.zeros((trial_rows, rank_size), jnp.float32),
         (blocks, neuron_blocks),
     )
-    quarter_sums = lax.psum(running, ("neuron", "tm"))
+    running, gram_time = lax.optimization_barrier((running, gram_time))
+    quarter_sums = tree_sum(running, ("neuron", "tm"))
+    inverse_trial = normal_inverse(gram_neuron * gram_time)
     raw_rows = apply_inverse(quarter_sums, inverse_trial)
-    squares = lax.psum(jnp.sum(raw_rows * raw_rows, axis=0), "trial")
+    squares = tree_sum(jnp.sum(raw_rows * raw_rows, axis=0), ("trial",))
     scales = jnp.sqrt(squares / trial_total + EPSILON)
     trial_local = (raw_rows / scales[None, :]).astype(jnp.bfloat16)
     return (neuron_own, time_local, trial_local)

time: 867 us -> 422 us (0.49)
  waiting for transfers between devices: 554 us -> 87.2 us
  starting transfers between devices: 0.21 us -> 56.6 us
  blocking collectives: 26.1 us -> 0 us
  between operations: 20.2 us -> 7.48 us
  local copies, waits for them, and re-layouts: 38.9 us -> 49.8 us
    psum x5 -> x0, waiting for transfers between devices: 554 us -> none  [the longest x1 212 us: on_device(): half_sums = lax.psum(running, ('neuron', 'trial'))]
    ppermute x0 -> x27, waiting for transfers between devices: none -> 87.2 us  [tree_sum(): values = values + lax.ppermute(values, axis, pairs)]
    ppermute x0 -> x27, starting transfers between devices: none -> 56.6 us  [tree_sum(): values = values + lax.ppermute(values, axis, pairs)]
    all_gather x2 -> x0, blocking collectives: 17.7 us -> none  [the longest x1 11 us: on_device(): trial_all = lax.all_gather(trial_factor, 'trial', axis=0, tiled=True)]
    mul x1 -> x2, local copies, waits for them, and re-layouts: 0.02 us -> 12 us  [mask_tensor(): return shaped * block_mask.astype(jnp.bfloat16)[:, None, None, :]]
  transfers between devices with their start and end apart: 5 -> 27, of which waited for: 4 -> 19; matrix products, arithmetic and copies ran while one was open for 10% -> 58% of each run, Pallas kernels for 0% -> 0%
where the time goes in v2:
time: 422 us; the launch traced here: 416 us
  other arithmetic  183 us (43%)
  waiting for transfers between devices  87.2 us (21%)
  starting transfers between devices  56.6 us (13%)
  local copies, waits for them, and re-layouts  49.8 us (12%)
  matrix products  31.2 us (7%)
  between operations  7.48 us (2%)
    another operation x20, other arithmetic, normal_inverse(): lower_factor = jnp.linalg.cholesky(scaled)  103 us
    ppermute x27, waiting for transfers between devices, tree_sum(): values = values + lax.ppermute(values, axis, pairs)  87.2 us
    another operation x7, other arithmetic, normal_inverse(): return jax.scipy.linalg.cho_solve((lower_factor, True), identity)  60 us
    ppermute x27, starting transfers between devices, tree_sum(): values = values + lax.ppermute(values, axis, pairs)  56.6 us
    mul x2, other arithmetic, mask_tensor(): return shaped * block_mask.astype(jnp.bfloat16)[:, None, None, :]  14.4 us
    unnamed x7, local copies, waits for them, and re-layouts  12.8 us
    mul x2, local copies, waits for them, and re-layouts, mask_tensor(): return shaped * block_mask.astype(jnp.bfloat16)[:, None, None, :]  12 us
    another operation x22, local copies, waits for them, and re-layouts, normal_inverse(): return jax.scipy.linalg.cho_solve((lower_factor, True), identity)  11.9 us
  transfers between devices with their start and end apart: 27, of which 19 were waited for; matrix products, arithmetic and copies ran while one was open for 58% of the time, Pallas kernels for 0%

profile of v2, /device:TPU:1, one launch (start us, length us, event | category | flops | bytes accessed | tf_op | source)
XLA Modules:
  0.0 415.8 jit_solution(1923875401041814878)
XLA Ops:
  8.9 7.2 %broadcast_multiply_fusion.1 = bf16[256,128,128]{2,1,0:T(8,128)(2,1)} fusion(bf16[256,128,128]{2,1,0:T(8,128)(2,1)} %param.12, bf16[256,128]{1,0:T(8,128)(2,1)S(1)} %bitcast.173), kind=kLoop, calls=%fused_computation.36 | loop fusion | flops 4194304 | bytes 16842752 | tf_op jit(solution)/shard_map/mul | solution.py:49
  16.1 12.0 %copy.26 = bf16[256,128,128]{1,0,2:T(8,128)(2,1)} copy(bf16[256,128,128]{2,1,0:T(8,128)(2,1)} %broadcast_multiply_fusion.1) | data formatting | bytes 16777216 | tf_op jit(solution)/shard_map/mul | solution.py:49
  46.0 11.7 %cholesky.172 = f32[128,128]{1,0:T(8,128)S(1)} custom-call(f32[128,128]{1,0:T(8,128)S(1)} %cholesky.270), custom_call_target="Cholesky" | custom-call | tf_op jit(solution)/shard_map/jit(cholesky)/cholesky | solution.py:14
  57.8 9.8 %custom-call.29 = f32[1,128,128]{1,2,0:T(8,128)S(1)} custom-call(f32[1,128,128]{2,1,0:T(8,128)S(1)} %get-tuple-element.217), custom_call_target="InvertDiagBlocksLowerTriangular" | custom-call | tf_op jit(solution)/shard_map/jit(cholesky)/cholesky | solution.py:14
  68.1 11.7 %cholesky.189 = f32[128,128]{1,0:T(8,128)S(1)} custom-call(f32[128,128]{1,0:T(8,128)S(1)} %convolution_subtract_fusion.8), custom_call_target="Cholesky" | custom-call | tf_op jit(solution)/shard_map/jit(cholesky)/cholesky | solution.py:14
  85.9 20.2 %custom-call.30 = f32[2,128,128]{1,2,0:T(8,128)S(1)} custom-call(f32[2,128,128]{2,1,0:T(8,128)S(1)} %get-tuple-element.125), custom_call_target="InvertDiagBlocksLowerTriangular" | custom-call | tf_op jit(solution)/shard_map/jit(_cho_solve)/triangular_solve | solution.py:15
  124.0 10.2 %collective-permute-done.7 = f32[256,256]{0,1:T(8,128)S(1)} collective-permute-done((f32[256,256]{0,1:T(8,128)S(1)}, f32[256,256]{0,1:T(8,128)S(1)}, u32[]{:S(2)}, u32[]{:S(2)}) %collective-permute-start.7) | collective-permute-done | bytes 262176 | tf_op jit(solution)/shard_map/ppermute | solution.py:58
  137.4 13.4 %collective-permute-done.8 = f32[256,256]{0,1:T(8,128)S(1)} collective-permute-done((f32[256,256]{0,1:T(8,128)S(1)}, f32[256,256]{0,1:T(8,128)S(1)}, u32[]{:S(2)}, u32[]{:S(2)}) %collective-permute-start.8) | collective-permute-done | bytes 262176 | tf_op jit(solution)/shard_map/ppermute | solution.py:58
  152.0 12.0 %copy.35 = bf16[256,128,128]{1,2,0:T(8,128)(2,1)} copy(bf16[256,128,128]{2,1,0:T(8,128)(2,1)} %param.12) | data formatting | bytes 16777216 | tf_op args[0]
  166.8 7.3 %broadcast_multiply_fusion = bf16[2,128,128,128]{2,3,1,0:T(8,128)(2,1)} fusion(bf16[2,128,128,128]{2,3,1,0:T(8,128)(2,1)} %bitcast.171, bf16[2,128]{1,0:T(2,128)(2,1)S(1)} %fusion.28), kind=kLoop, calls=%fused_computation.35 | loop fusion | flops 4194304 | bytes 16777728 | tf_op jit(solution)/shard_map/mul | solution.py:49
  176.8 7.4 %while.28 = (s32[]{:T(128)}, f32[128,256]{1,0:T(8,128)S(1)}, bf16[2,128,128,128]{2,3,1,0:T(8,128)(2,1)}, bf16[2,128,256]{2,1,0:T(8,128)(2,1)S(1)}, bf16[128,256]{1,0:T(8,128)(2,1)S(1)}, /*index=5*/s32[]{:T(128)}, s32[]{:T(128)}) while((s32[]{:T(128)}, f32[128,256]{1,0:T(8,128)S(1)}, bf16[2,128,128,128]{2,3,1,0:T(8,128)(2,1)}, ...), condition=%wide.region_6.9_spmd.clone, body=%wide.region_5.8_spmd.clone.sunk | while | flops 1082261504 | bytes 5112411 | solution.py:100
  188.4 11.7 %cholesky.206 = f32[128,128]{1,0:T(8,128)S(1)} custom-call(f32[128,128]{1,0:T(8,128)S(1)} %cholesky.273), custom_call_target="Cholesky" | custom-call | tf_op jit(solution)/shard_map/jit(cholesky)/cholesky | solution.py:14
  200.2 9.8 %custom-call.31 = f32[1,128,128]{1,2,0:T(8,128)S(1)} custom-call(f32[1,128,128]{2,1,0:T(8,128)S(1)} %get-tuple-element.213), custom_call_target="InvertDiagBlocksLowerTriangular" | custom-call | tf_op jit(solution)/shard_map/jit(cholesky)/cholesky | solution.py:14
  210.5 11.7 %cholesky.223 = f32[128,128]{1,0:T(8,128)S(1)} custom-call(f32[128,128]{1,0:T(8,128)S(1)} %convolution_subtract_fusion.7), custom_call_target="Cholesky" | custom-call | tf_op jit(solution)/shard_map/jit(cholesky)/cholesky | solution.py:14
  228.9 19.9 %custom-call.32 = f32[2,128,128]{1,2,0:T(8,128)S(1)} custom-call(f32[2,128,128]{2,1,0:T(8,128)S(1)} %get-tuple-element.126), custom_call_target="InvertDiagBlocksLowerTriangular" | custom-call | tf_op jit(solution)/shard_map/jit(_cho_solve)/triangular_solve | solution.py:15
  255.6 7.3 %collective-permute-done.13 = f32[128,256]{1,0:T(8,128)S(1)} collective-permute-done((f32[128,256]{1,0:T(8,128)S(1)}, f32[128,256]{1,0:T(8,128)S(1)}, u32[]{:S(2)}, u32[]{:S(2)}) %collective-permute-start.13) | collective-permute-done | bytes 131104 | tf_op jit(solution)/shard_map/ppermute | solution.py:58
  282.6 15.6 %collective-permute-start.18 = (f32[256,256]{0,1:T(8,128)S(1)}, f32[256,256]{0,1:T(8,128)S(1)}, u32[]{:S(2)}, u32[]{:S(2)}) collective-permute-start(f32[256,256]{0,1:T(8,128)S(1)} %fusion.89), channel_id=1, source_target_pairs={{0,4},{4,0},{1,5},{5,1},{2,6},{6,2},{3,7},{7,3},{8,12},{12,8},{9,1... | collective-permute-start | bytes 786440 | tf_op jit(solution)/shard_map/ppermute | solution.py:58
  302.0 7.2 %while.29 = (s32[]{:T(128)}, f32[128,256]{1,0:T(8,128)S(1)}, bf16[2,128,128,128]{2,3,1,0:T(8,128)(2,1)}, bf16[2,128,256]{2,1,0:T(8,128)(2,1)S(1)}, bf16[128,256]{1,0:T(8,128)(2,1)S(1)}, /*index=5*/s32[]{:T(128)}, s32[]{:T(128)}) while((s32[]{:T(128)}, f32[128,256]{1,0:T(8,128)S(1)}, bf16[2,128,128,128]{2,3,1,0:T(8,128)(2,1)}, ...), condition=%wide.region_9.12_spmd.clone, body=%wide.region_8.11_spmd.clone.sunk | while | flops 1082261504 | bytes 5112411 | solution.py:122
  313.6 11.7 %cholesky.240 = f32[128,128]{1,0:T(8,128)S(1)} custom-call(f32[128,128]{1,0:T(8,128)S(1)} %cholesky.276), custom_call_target="Cholesky" | custom-call | tf_op jit(solution)/shard_map/jit(cholesky)/cholesky | solution.py:14
  325.4 9.8 %custom-call.33 = f32[1,128,128]{1,2,0:T(8,128)S(1)} custom-call(f32[1,128,128]{2,1,0:T(8,128)S(1)} %get-tuple-element.209), custom_call_target="InvertDiagBlocksLowerTriangular" | custom-call | tf_op jit(solution)/shard_map/jit(cholesky)/cholesky | solution.py:14
  335.7 11.7 %cholesky.257 = f32[128,128]{1,0:T(8,128)S(1)} custom-call(f32[128,128]{1,0:T(8,128)S(1)} %convolution_subtract_fusion.6), custom_call_target="Cholesky" | custom-call | tf_op jit(solution)/shard_map/jit(cholesky)/cholesky | solution.py:14
  354.1 19.8 %custom-call.34 = f32[2,128,128]{1,2,0:T(8,128)S(1)} custom-call(f32[2,128,128]{2,1,0:T(8,128)S(1)} %get-tuple-element.127), custom_call_target="InvertDiagBlocksLowerTriangular" | custom-call | tf_op jit(solution)/shard_map/jit(_cho_solve)/triangular_solve | solution.py:15
  376.1 6.6 %collective-permute-done.20 = f32[128,256]{1,0:T(8,128)S(1)} collective-permute-done((f32[128,256]{1,0:T(8,128)S(1)}, f32[128,256]{1,0:T(8,128)S(1)}, u32[]{:S(2)}, u32[]{:S(2)}) %collective-permute-start.20) | collective-permute-done | bytes 131104 | tf_op jit(solution)/shard_map/ppermute | solution.py:58
  400.4 6.8 %collective-permute-start.24 = (f32[128,256]{1,0:T(8,128)S(1)}, f32[128,256]{1,0:T(8,128)S(1)}, u32[]{:S(2)}, u32[]{:S(2)}) collective-permute-start(f32[128,256]{1,0:T(8,128)S(1)} %add.194), channel_id=1, source_target_pairs={{0,4},{4,0},{1,5},{5,1},{2,6},{6,2},{3,7},{7,3},{8,12},{12,8},{9,1... | collective-permute-start | bytes 393224 | tf_op jit(solution)/shard_map/ppermute | solution.py:58
  (202 shorter events, 162.0 us)
Async XLA Ops:
  1.8 31.3 %collective-permute-start.4 = (f32[256,256]{0,1:T(8,128)S(1)}, f32[256,256]{0,1:T(8,128)S(1)}, u32[]{:S(2)}, u32[]{:S(2)}) collective-permute-start(f32[256,256]{0,1:T(8,128)S(1)} %fusion.87), channel_id=1, source_target_pairs={{0,1},{1,0},{2,3},{3,2},{4,5},{5,4},{6,7},{7,6},{8,9},{9,8},{10,11... | collective-permute-start | bytes 786440 | tf_op jit(solution)/shard_map/ppermute | solution.py:58
  5.0 31.7 %collective-permute-start.3 = (f32[256,256]{0,1:T(8,128)S(1)}, f32[256,256]{0,1:T(8,128)S(1)}, u32[]{:S(2)}, u32[]{:S(2)}) collective-permute-start(f32[256,256]{0,1:T(8,128)S(1)} %fusion.86), channel_id=1, source_target_pairs={{0,4},{4,0},{1,5},{5,1},{2,6},{6,2},{3,7},{7,3},{8,12},{12,8},{9,1... | collective-permute-start | bytes 786440 | tf_op jit(solution)/shard_map/ppermute | solution.py:58
  33.1 9.0 %collective-permute-start.5 = (f32[256,256]{0,1:T(8,128)S(1)}, f32[256,256]{0,1:T(8,128)S(1)}, u32[]{:S(2)}, u32[]{:S(2)}) collective-permute-start(f32[256,256]{0,1:T(8,128)S(1)} %add.169), channel_id=1, source_target_pairs={{0,2},{1,3},{2,0},{3,1},{4,6},{5,7},{6,4},{7,5},{8,10},{9,11},{10,... | collective-permute-start | bytes 786440 | tf_op jit(solution)/shard_map/ppermute | solution.py:58
  35.5 71.9 %collective-permute-start.1 = (f32[256,256]{1,0:T(8,128)S(1)}, f32[256,256]{1,0:T(8,128)S(1)}, u32[]{:S(2)}, u32[]{:S(2)}) collective-permute-start(f32[256,256]{1,0:T(8,128)S(1)} %add.165), channel_id=1, source_target_pairs={{0,1},{1,0},{2,3},{3,2},{4,5},{5,4},{6,7},{7,6},{8,9},{9,8},{10,11... | collective-permute-start | bytes 786440 | tf_op jit(solution)/shard_map/ppermute | solution.py:58
  107.5 7.2 %collective-permute-start.2 = (f32[256,256]{1,0:T(8,128)S(1)}, f32[256,256]{1,0:T(8,128)S(1)}, u32[]{:S(2)}, u32[]{:S(2)}) collective-permute-start(f32[256,256]{1,0:T(8,128)S(1)} %add.166), channel_id=1, source_target_pairs={{0,2},{1,3},{2,0},{3,1},{4,6},{5,7},{6,4},{7,5},{8,10},{9,11},{10,... | collective-permute-start | bytes 786440 | tf_op jit(solution)/shard_map/ppermute | solution.py:58
  115.6 5.3 %collective-permute-start.6 = (f32[256,256]{0,1:T(8,128)S(1)}, f32[256,256]{0,1:T(8,128)S(1)}, u32[]{:S(2)}, u32[]{:S(2)}) collective-permute-start(f32[256,256]{0,1:T(8,128)S(1)} %fusion.88), channel_id=1, source_target_pairs={{0,8},{8,0},{16,24},{24,16},{32,40},{40,32},{48,56},{56,48},{64,72... | collective-permute-start | bytes 786440 | tf_op jit(solution)/shard_map/ppermute | solution.py:58
  121.0 13.2 %collective-permute-start.7 = (f32[256,256]{0,1:T(8,128)S(1)}, f32[256,256]{0,1:T(8,128)S(1)}, u32[]{:S(2)}, u32[]{:S(2)}) collective-permute-start(f32[256,256]{0,1:T(8,128)S(1)} %add.172), channel_id=1, source_target_pairs={{0,16},{8,24},{16,0},{24,8},{32,48},{40,56},{48,32},{56,40},{64,80... | collective-permute-start | bytes 786440 | tf_op jit(solution)/shard_map/ppermute | solution.py:58
  134.2 16.5 %collective-permute-start.8 = (f32[256,256]{0,1:T(8,128)S(1)}, f32[256,256]{0,1:T(8,128)S(1)}, u32[]{:S(2)}, u32[]{:S(2)}) collective-permute-start(f32[256,256]{0,1:T(8,128)S(1)} %add.173), channel_id=1, source_target_pairs={{0,32},{8,40},{16,48},{24,56},{32,0},{40,8},{48,16},{56,24},{64,96... | collective-permute-start | bytes 786440 | tf_op jit(solution)/shard_map/ppermute | solution.py:58
  150.8 13.2 %collective-permute-start.9 = (f32[256,256]{0,1:T(8,128)S(1)}, f32[256,256]{0,1:T(8,128)S(1)}, u32[]{:S(2)}, u32[]{:S(2)}) collective-permute-start(f32[256,256]{0,1:T(8,128)S(1)} %add.174), channel_id=1, source_target_pairs={{0,64},{8,72},{16,80},{24,88},{32,96},{40,104},{48,112},{56,120},{... | collective-permute-start | bytes 786440 | tf_op jit(solution)/shard_map/ppermute | solution.py:58
  164.0 10.1 %collective-permute-start.10 = (f32[256,256]{0,1:T(8,128)S(1)}, f32[256,256]{0,1:T(8,128)S(1)}, u32[]{:S(2)}, u32[]{:S(2)}) collective-permute-start(f32[256,256]{0,1:T(8,128)S(1)} %add.175), channel_id=1, source_target_pairs={{0,128},{8,136},{16,144},{24,152},{32,160},{40,168},{48,176},{56,1... | collective-permute-start | bytes 786440 | tf_op jit(solution)/shard_map/ppermute | solution.py:58
  184.2 64.6 %collective-permute-start.11 = (f32[128,256]{1,0:T(8,128)S(1)}, f32[128,256]{1,0:T(8,128)S(1)}, u32[]{:S(2)}, u32[]{:S(2)}) collective-permute-start(f32[128,256]{1,0:T(8,128)S(1)} %get-tuple-element.64), channel_id=1, source_target_pairs={{0,8},{8,0},{16,24},{24,16},{32,40},{40,32},{48,56},{56,48},{64,72... | collective-permute-start | bytes 393224 | tf_op jit(solution)/shard_map/ppermute | solution.py:58
  248.8 6.2 %collective-permute-start.12 = (f32[128,256]{1,0:T(8,128)S(1)}, f32[128,256]{1,0:T(8,128)S(1)}, u32[]{:S(2)}, u32[]{:S(2)}) collective-permute-start(f32[128,256]{1,0:T(8,128)S(1)} %add.180), channel_id=1, source_target_pairs={{0,16},{8,24},{16,0},{24,8},{32,48},{40,56},{48,32},{56,40},{64,80... | collective-permute-start | bytes 393224 | tf_op jit(solution)/shard_map/ppermute | solution.py:58
  255.1 7.8 %collective-permute-start.13 = (f32[128,256]{1,0:T(8,128)S(1)}, f32[128,256]{1,0:T(8,128)S(1)}, u32[]{:S(2)}, u32[]{:S(2)}) collective-permute-start(f32[128,256]{1,0:T(8,128)S(1)} %add.181), channel_id=1, source_target_pairs={{0,32},{8,40},{16,48},{24,56},{32,0},{40,8},{48,16},{56,24},{64,96... | collective-permute-start | bytes 393224 | tf_op jit(solution)/shard_map/ppermute | solution.py:58
  262.9 3.9 collective-permute-start.14
  266.8 5.7 %collective-permute-start.15 = (f32[128,256]{1,0:T(8,128)S(1)}, f32[128,256]{1,0:T(8,128)S(1)}, u32[]{:S(2)}, u32[]{:S(2)}) collective-permute-start(f32[128,256]{1,0:T(8,128)S(1)} %add.183), channel_id=1, source_target_pairs={{0,128},{8,136},{16,144},{24,152},{32,160},{40,168},{48,176},{56,1... | collective-permute-start | bytes 393224 | tf_op jit(solution)/shard_map/ppermute | solution.py:58
  276.5 5.4 %collective-permute-start.17 = (f32[128,256]{1,0:T(8,128)S(1)}, f32[128,256]{1,0:T(8,128)S(1)}, u32[]{:S(2)}, u32[]{:S(2)}) collective-permute-start(f32[128,256]{1,0:T(8,128)S(1)} %add.185), channel_id=1, source_target_pairs={{0,2},{1,3},{2,0},{3,1},{4,6},{5,7},{6,4},{7,5},{8,10},{9,11},{10,... | collective-permute-start | bytes 393224 | tf_op jit(solution)/shard_map/ppermute | solution.py:58
  282.6 16.8 %collective-permute-start.18 = (f32[256,256]{0,1:T(8,128)S(1)}, f32[256,256]{0,1:T(8,128)S(1)}, u32[]{:S(2)}, u32[]{:S(2)}) collective-permute-start(f32[256,256]{0,1:T(8,128)S(1)} %fusion.89), channel_id=1, source_target_pairs={{0,4},{4,0},{1,5},{5,1},{2,6},{6,2},{3,7},{7,3},{8,12},{12,8},{9,1... | collective-permute-start | bytes 786440 | tf_op jit(solution)/shard_map/ppermute | solution.py:58
  309.2 65.1 %collective-permute-start.19 = (f32[128,256]{1,0:T(8,128)S(1)}, f32[128,256]{1,0:T(8,128)S(1)}, u32[]{:S(2)}, u32[]{:S(2)}) collective-permute-start(f32[128,256]{1,0:T(8,128)S(1)} %get-tuple-element.67), channel_id=1, source_target_pairs={{0,8},{8,0},{16,24},{24,16},{32,40},{40,32},{48,56},{56,48},{64,72... | collective-permute-start | bytes 393224 | tf_op jit(solution)/shard_map/ppermute | solution.py:58
  374.3 8.5 %collective-permute-start.20 = (f32[128,256]{1,0:T(8,128)S(1)}, f32[128,256]{1,0:T(8,128)S(1)}, u32[]{:S(2)}, u32[]{:S(2)}) collective-permute-start(f32[128,256]{1,0:T(8,128)S(1)} %add.190), channel_id=1, source_target_pairs={{0,16},{8,24},{16,0},{24,8},{32,48},{40,56},{48,32},{56,40},{64,80... | collective-permute-start | bytes 393224 | tf_op jit(solution)/shard_map/ppermute | solution.py:58
  382.8 7.9 %collective-permute-start.21 = (f32[128,256]{1,0:T(8,128)S(1)}, f32[128,256]{1,0:T(8,128)S(1)}, u32[]{:S(2)}, u32[]{:S(2)}) collective-permute-start(f32[128,256]{1,0:T(8,128)S(1)} %add.191), channel_id=1, source_target_pairs={{0,32},{8,40},{16,48},{24,56},{32,0},{40,8},{48,16},{56,24},{64,96... | collective-permute-start | bytes 393224 | tf_op jit(solution)/shard_map/ppermute | solution.py:58
  390.7 4.2 %collective-permute-start.22 = (f32[128,256]{1,0:T(8,128)S(1)}, f32[128,256]{1,0:T(8,128)S(1)}, u32[]{:S(2)}, u32[]{:S(2)}) collective-permute-start(f32[128,256]{1,0:T(8,128)S(1)} %add.192), channel_id=1, source_target_pairs={{0,64},{8,72},{16,80},{24,88},{32,96},{40,104},{48,112},{56,120},{... | collective-permute-start | bytes 393224 | tf_op jit(solution)/shard_map/ppermute | solution.py:58
  395.0 5.4 %collective-permute-start.23 = (f32[128,256]{1,0:T(8,128)S(1)}, f32[128,256]{1,0:T(8,128)S(1)}, u32[]{:S(2)}, u32[]{:S(2)}) collective-permute-start(f32[128,256]{1,0:T(8,128)S(1)} %add.193), channel_id=1, source_target_pairs={{0,128},{8,136},{16,144},{24,152},{32,160},{40,168},{48,176},{56,1... | collective-permute-start | bytes 393224 | tf_op jit(solution)/shard_map/ppermute | solution.py:58
  400.4 7.8 %collective-permute-start.24 = (f32[128,256]{1,0:T(8,128)S(1)}, f32[128,256]{1,0:T(8,128)S(1)}, u32[]{:S(2)}, u32[]{:S(2)}) collective-permute-start(f32[128,256]{1,0:T(8,128)S(1)} %add.194), channel_id=1, source_target_pairs={{0,4},{4,0},{1,5},{5,1},{2,6},{6,2},{3,7},{7,3},{8,12},{12,8},{9,1... | collective-permute-start | bytes 393224 | tf_op jit(solution)/shard_map/ppermute | solution.py:58
  411.0 3.9 collective-permute-start.26
  (5 other events, 125.4 us)

commit v3 on v2

--- a/solution.py
+++ b/solution.py
@@ -12,11 +12,12 @@
     identity = jnp.eye(order_size, dtype=jnp.float32)
     scaled = gram_matrix / jnp.mean(jnp.diagonal(gram_matrix)) + RIDGE * identity
     lower_factor = jnp.linalg.cholesky(scaled)
-    return jax.scipy.linalg.cho_solve((lower_factor, True), identity)
+    return lax.linalg.triangular_solve(lower_factor, identity, left_side=True, lower=True)
 
 
-def apply_inverse(partial_sums, inverse):
-    return jnp.dot(partial_sums, inverse, precision=lax.Precision.HIGHEST)
+def apply_inverse(partial_sums, inverse_factor):
+    half = jnp.dot(partial_sums, inverse_factor.T, precision=lax.Precision.HIGHEST)
+    return jnp.dot(half, inverse_factor, precision=lax.Precision.HIGHEST)
 
 
 def raw_gram(raw_rows):
@@ -36,17 +37,12 @@
     return (factor, normed)
 
 
-def mask_tensor(tensor, present_blocks, trial_day):
+def block_mask_of(present_blocks, trial_day):
     day_count = present_blocks.shape[1]
     onehot = (trial_day[:, None] == jnp.arange(day_count, dtype=jnp.int32)[None, :]).astype(
         jnp.float32
     )
-    block_mask = jnp.dot(present_blocks.astype(jnp.float32), onehot.T)
-    block_count = present_blocks.shape[0]
-    shaped = tensor.reshape(
-        block_count, tensor.shape[0] // block_count, tensor.shape[1], tensor.shape[2]
-    )
-    return shaped * block_mask.astype(jnp.bfloat16)[:, None, None, :]
+    return jnp.dot(present_blocks.astype(jnp.float32), onehot.T).astype(jnp.bfloat16)
 
 
 def tree_sum(values, axes):
@@ -65,18 +61,22 @@
 
 
 def on_device(tensor, present_blocks, trial_day, time_factor, trial_factor):
-    blocks = mask_tensor(tensor, present_blocks, trial_day)
-    block_count, block_rows, time_rows, trial_rows = blocks.shape
-    neuron_rows = block_count * block_rows
-    flattened = blocks.reshape(neuron_rows, time_rows, trial_rows)
+    block_mask = block_mask_of(present_blocks, trial_day)
+    block_count = present_blocks.shape[0]
+    neuron_rows, time_rows, trial_rows = tensor.shape
+    block_rows = neuron_rows // block_count
+    blocks = tensor.reshape(block_count, block_rows, time_rows, trial_rows)
     rank_size = time_factor.shape[1]
     start_time = tree_sum(factor_gram(time_factor), ("tm",))
     start_trial = tree_sum(factor_gram(trial_factor), ("trial",))
     inverse_neuron = normal_inverse(start_time * start_trial)
     kr_tk = khatri_rao(time_factor, trial_factor)
     neuron_total = neuron_rows * lax.axis_size("neuron")
+    kr_masked = kr_tk[None, :, :, :] * block_mask[:, None, :, None]
     block_sums = tree_sum(
-        jnp.einsum("itk,tkr->ir", flattened, kr_tk, preferred_element_type=jnp.float32),
+        jnp.einsum(
+            "bitk,btkr->bir", blocks, kr_masked, preferred_element_type=jnp.float32
+        ).reshape(neuron_rows, rank_size),
         ("tm", "trial"),
     )
     raw_rows = apply_inverse(block_sums, inverse_neuron)
@@ -89,8 +89,8 @@
     time_total = time_rows * lax.axis_size("tm")
 
     def time_add_block(running, inputs):
-        tensor_piece, rows_a = inputs
-        kr_ik = khatri_rao(rows_a, trial_factor)
+        tensor_piece, mask_row, rows_a = inputs
+        kr_ik = khatri_rao(rows_a, trial_factor) * mask_row[None, :, None]
         return (
             running
             + jnp.einsum("itk,ikr->tr", tensor_piece, kr_ik, preferred_element_type=jnp.float32),
@@ -100,7 +100,7 @@
     running, unused = lax.scan(
         time_add_block,
         jnp.zeros((time_rows, rank_size), jnp.float32),
-        (blocks, neuron_blocks),
+        (blocks, block_mask, neuron_blocks),
     )
     running, gram_neuron = lax.optimization_barrier((running, gram_neuron))
     half_sums = tree_sum(running, ("neuron", "trial"))
@@ -111,18 +111,17 @@
     trial_total = trial_rows * lax.axis_size("trial")
 
     def trial_add_block(running, inputs):
-        tensor_piece, rows_a = inputs
+        tensor_piece, mask_row, rows_a = inputs
         kr_it = khatri_rao(rows_a, time_local)
-        return (
-            running
-            + jnp.einsum("itk,itr->kr", tensor_piece, kr_it, preferred_element_type=jnp.float32),
-            None,
+        block_part = jnp.einsum(
+            "itk,itr->kr", tensor_piece, kr_it, preferred_element_type=jnp.float32
         )
+        return (running + block_part * mask_row.astype(jnp.float32)[:, None], None)
 
     running, unused = lax.scan(
         trial_add_block,
         jnp.zeros((trial_rows, rank_size), jnp.float32),
-        (blocks, neuron_blocks),
+        (blocks, block_mask, neuron_blocks),
     )
     running, gram_time = lax.optimization_barrier((running, gram_time))
     quarter_sums = tree_sum(running, ("neuron", "tm"))

time: 422 us -> 422 us (level)
  other arithmetic: 183 us -> 173 us
  starting transfers between devices: 56.6 us -> 62.1 us
    mul x2 -> x0, other arithmetic: 14.4 us -> none  [mask_tensor(): return shaped * block_mask.astype(jnp.bfloat16)[:, None, None, :]]
    reshape x0 -> x1, local copies, waits for them, and re-layouts: none -> 12.4 us  [on_device(): blocks = tensor.reshape(block_count, block_rows, time_rows, trial_rows)]
    mul x2, local copies, waits for them, and re-layouts: 12 us -> 0.02 us  [time_add_block(): kr_ik = khatri_rao(rows_a, trial_factor) * mask_row[None, :, None]]
    convert_element_type x0 -> x3, other arithmetic: none -> 6.76 us  [the longest x1 6.74 us: khatri_rao(): return (left_rows.astype(jnp.float32)[:, None, :] * right_rows.astype(jnp...]
    ppermute x27, starting transfers between devices: 56.6 us -> 62.1 us  [tree_sum(): values = values + lax.ppermute(values, axis, pairs)]
    dot_general x5 -> x8, matrix products: 6.73 us -> 10.6 us  [the longest x1 8.27 us: on_device(): jnp.einsum('bitk,btkr->bir', blocks, kr_masked, preferred_element_type=jn...]
    unnamed x7 -> x13, local copies, waits for them, and re-layouts: 12.8 us -> 12.8 us
  transfers between devices with their start and end apart: 27 -> 27, of which waited for: 19 -> 22; matrix products, arithmetic and copies ran while one was open for 58% -> 31% of each run, Pallas kernels for 0% -> 0%
where the time goes in v3:
time: 422 us; the launch traced here: 414 us
  other arithmetic  173 us (41%)
  waiting for transfers between devices  89.4 us (21%)
  starting transfers between devices  62.1 us (15%)
  local copies, waits for them, and re-layouts  49.9 us (12%)
  matrix products  31.5 us (7%)
  between operations  7.4 us (2%)
    another operation x20, other arithmetic, normal_inverse(): lower_factor = jnp.linalg.cholesky(scaled)  103 us
    ppermute x27, waiting for transfers between devices, tree_sum(): values = values + lax.ppermute(values, axis, pairs)  89.4 us
    ppermute x27, starting transfers between devices, tree_sum(): values = values + lax.ppermute(values, axis, pairs)  62.1 us
    another operation x7, other arithmetic, normal_inverse(): lax.linalg.triangular_solve(lower_factor, identity, left_side=True, lower...  59.3 us
    unnamed x13, local copies, waits for them, and re-layouts  12.8 us
    reshape x1, local copies, waits for them, and re-layouts, on_device(): blocks = tensor.reshape(block_count, block_rows, time_rows, trial_rows)  12.4 us
    another operation x22, local copies, waits for them, and re-layouts, normal_inverse(): lax.linalg.triangular_solve(lower_factor, identity, left_side=True, lower...  11.8 us
  transfers between devices with their start and end apart: 27, of which 22 were waited for; matrix products, arithmetic and copies ran while one was open for 31% of the time, Pallas kernels for 0%

profile of v3, /device:TPU:1, one launch (start us, length us, event | category | flops | bytes accessed | tf_op | source)
XLA Modules:
  0.0 413.8 jit_solution(6279461700666928576)
XLA Ops:
  0.7 12.4 %copy.27 = bf16[2,128,128,128]{2,1,3,0:T(8,128)(2,1)} copy(bf16[2,128,128,128]{3,2,1,0:T(8,128)(2,1)} %bitcast.179) | data formatting | bytes 16777216 | tf_op jit(solution)/shard_map/reshape | solution.py:68
  13.3 6.7 %multiply_convert_fusion.9 = bf16[128,128,256]{2,0,1:T(8,128)(2,1)} fusion(f32[128,256]{1,0:T(8,128)S(1)} %convert_element_type.92, f32[128,256]{1,0:T(8,128)S(1)} %convert_element_type.91), kind=kLoop, calls=%fused_computation.41 | loop fusion | flops 8388608 | bytes 8650752 | tf_op jit(solution)/shard_map/convert_element_type | solution.py:30
  20.1 8.3 %fusion.37 = f32[2,256,128,1]{1,2,3,0:T(8,128)S(1)} fusion(bf16[2,128,128,128]{2,1,3,0:T(8,128)(2,1)} %copy.27, bf16[2,128]{1,0:T(2,128)(2,1)S(1)} %fusion.41, bf16[128,128,256]{2,0,1:T(8,128)(2,1)} %multiply_convert_fusion.9), kind=kOutput, calls=%fused_computation.39 | convolution fusion | flops 2181038080 | bytes 17039872 | tf_op jit(solution)/shard_map/bitk,btkr->bir/dot_general | solution.py:77
  55.5 11.7 %cholesky.172 = f32[128,128]{1,0:T(8,128)S(1)} custom-call(f32[128,128]{1,0:T(8,128)S(1)} %cholesky.270), custom_call_target="Cholesky" | custom-call | tf_op jit(solution)/shard_map/jit(cholesky)/cholesky | solution.py:14
  67.3 9.8 %custom-call.27 = f32[1,128,128]{1,2,0:T(8,128)S(1)} custom-call(f32[1,128,128]{2,1,0:T(8,128)S(1)} %get-tuple-element.241), custom_call_target="InvertDiagBlocksLowerTriangular" | custom-call | tf_op jit(solution)/shard_map/jit(cholesky)/cholesky | solution.py:14
  77.6 11.7 %cholesky.189 = f32[128,128]{1,0:T(8,128)S(1)} custom-call(f32[128,128]{1,0:T(8,128)S(1)} %convolution_subtract_fusion.5), custom_call_target="Cholesky" | custom-call | tf_op jit(solution)/shard_map/jit(cholesky)/cholesky | solution.py:14
  95.4 19.8 %custom-call.28 = f32[2,128,128]{1,2,0:T(8,128)S(1)} custom-call(f32[2,128,128]{2,1,0:T(8,128)S(1)} %get-tuple-element.141), custom_call_target="InvertDiagBlocksLowerTriangular" | custom-call | tf_op jit(solution)/shard_map/triangular_solve/custom-call.0 | solution.py:15
  127.8 11.4 %collective-permute-done.7 = f32[256,256]{0,1:T(8,128)S(1)} collective-permute-done((f32[256,256]{0,1:T(8,128)S(1)}, f32[256,256]{0,1:T(8,128)S(1)}, u32[]{:S(2)}, u32[]{:S(2)}) %collective-permute-start.7) | collective-permute-done | bytes 262176 | tf_op jit(solution)/shard_map/ppermute | solution.py:54
  139.2 6.6 %collective-permute-start.8 = (f32[256,256]{0,1:T(8,128)S(1)}, f32[256,256]{0,1:T(8,128)S(1)}, u32[]{:S(2)}, u32[]{:S(2)}) collective-permute-start(f32[256,256]{0,1:T(8,128)S(1)} %add.170), channel_id=1, source_target_pairs={{0,32},{8,40},{16,48},{24,56},{32,0},{40,8},{48,16},{56,24},{64,96... | collective-permute-start | bytes 786440 | tf_op jit(solution)/shard_map/ppermute | solution.py:54
  145.8 8.7 %collective-permute-done.8 = f32[256,256]{0,1:T(8,128)S(1)} collective-permute-done((f32[256,256]{0,1:T(8,128)S(1)}, f32[256,256]{0,1:T(8,128)S(1)}, u32[]{:S(2)}, u32[]{:S(2)}) %collective-permute-start.8) | collective-permute-done | bytes 262176 | tf_op jit(solution)/shard_map/ppermute | solution.py:54
  163.0 6.1 %collective-permute-done.10 = f32[256,256]{0,1:T(8,128)S(1)} collective-permute-done((f32[256,256]{0,1:T(8,128)S(1)}, f32[256,256]{0,1:T(8,128)S(1)}, u32[]{:S(2)}, u32[]{:S(2)}) %collective-permute-start.10) | collective-permute-done | bytes 262176 | tf_op jit(solution)/shard_map/ppermute | solution.py:54
  171.8 8.1 %while.28 = (s32[]{:T(128)}, f32[128,256]{1,0:T(8,128)S(1)}, bf16[2,128,128,128]{3,2,1,0:T(8,128)(2,1)}, bf16[2,128,256]{2,1,0:T(8,128)(2,1)S(1)}, bf16[128,256]...) while((s32[]{:T(128)}, f32[128,256]{1,0:T(8,128)S(1)}, ...), condition=%wide.region_6.9_spmd.clone, body=%wide.region_5.8_spmd.clone.sunk | while | flops 1086455808 | bytes 5112691 | solution.py:100
  184.0 11.7 %cholesky.206 = f32[128,128]{1,0:T(8,128)S(1)} custom-call(f32[128,128]{1,0:T(8,128)S(1)} %cholesky.273), custom_call_target="Cholesky" | custom-call | tf_op jit(solution)/shard_map/jit(cholesky)/cholesky | solution.py:14
  195.8 9.8 %custom-call.29 = f32[1,128,128]{1,2,0:T(8,128)S(1)} custom-call(f32[1,128,128]{2,1,0:T(8,128)S(1)} %get-tuple-element.237), custom_call_target="InvertDiagBlocksLowerTriangular" | custom-call | tf_op jit(solution)/shard_map/jit(cholesky)/cholesky | solution.py:14
  206.1 11.7 %cholesky.223 = f32[128,128]{1,0:T(8,128)S(1)} custom-call(f32[128,128]{1,0:T(8,128)S(1)} %convolution_subtract_fusion.4), custom_call_target="Cholesky" | custom-call | tf_op jit(solution)/shard_map/jit(cholesky)/cholesky | solution.py:14
  244.0 19.7 %custom-call.30 = f32[2,128,128]{1,2,0:T(8,128)S(1)} custom-call(f32[2,128,128]{2,1,0:T(8,128)S(1)} %get-tuple-element.142), custom_call_target="InvertDiagBlocksLowerTriangular" | custom-call | tf_op jit(solution)/shard_map/triangular_solve/custom-call.0 | solution.py:15
  279.6 11.1 %collective-permute-start.18 = (f32[256,256]{0,1:T(8,128)S(1)}, f32[256,256]{0,1:T(8,128)S(1)}, u32[]{:S(2)}, u32[]{:S(2)}) collective-permute-start(f32[256,256]{0,1:T(8,128)S(1)} %fusion.90), channel_id=1, source_target_pairs={{0,4},{4,0},{1,5},{5,1},{2,6},{6,2},{3,7},{7,3},{8,12},{12,8},{9,1... | collective-permute-start | bytes 786440 | tf_op jit(solution)/shard_map/ppermute | solution.py:54
  290.7 12.0 %copy.26 = bf16[256,128,128]{1,2,0:T(8,128)(2,1)} copy(bf16[256,128,128]{2,1,0:T(8,128)(2,1)} %bitcast.181) | data formatting | bytes 16777216 | tf_op args[0]
  305.2 7.2 %while.29 = (s32[]{:T(128)}, f32[128,256]{1,0:T(8,128)S(1)}, bf16[2,128,128,128]{2,3,1,0:T(8,128)(2,1)}, bf16[2,128,256]{2,1,0:T(8,128)(2,1)S(1)}, bf16[128,256]...) while((s32[]{:T(128)}, f32[128,256]{1,0:T(8,128)S(1)}, ...), condition=%wide.region_9.12_spmd.clone, body=%wide.region_8.11_spmd.clone.sunk | while | flops 1082294400 | bytes 5113203 | solution.py:121
  316.6 11.7 %cholesky.240 = f32[128,128]{1,0:T(8,128)S(1)} custom-call(f32[128,128]{1,0:T(8,128)S(1)} %cholesky.276), custom_call_target="Cholesky" | custom-call | tf_op jit(solution)/shard_map/jit(cholesky)/cholesky | solution.py:14
  328.4 9.8 %custom-call.31 = f32[1,128,128]{1,2,0:T(8,128)S(1)} custom-call(f32[1,128,128]{2,1,0:T(8,128)S(1)} %get-tuple-element.233), custom_call_target="InvertDiagBlocksLowerTriangular" | custom-call | tf_op jit(solution)/shard_map/jit(cholesky)/cholesky | solution.py:14
  338.7 11.7 %cholesky.257 = f32[128,128]{1,0:T(8,128)S(1)} custom-call(f32[128,128]{1,0:T(8,128)S(1)} %convolution_subtract_fusion.3), custom_call_target="Cholesky" | custom-call | tf_op jit(solution)/shard_map/jit(cholesky)/cholesky | solution.py:14
  357.0 7.7 %collective-permute-done.20 = f32[128,256]{1,0:T(8,128)S(1)} collective-permute-done((f32[128,256]{1,0:T(8,128)S(1)}, f32[128,256]{1,0:T(8,128)S(1)}, u32[]{:S(2)}, u32[]{:S(2)}) %collective-permute-start.20) | collective-permute-done | bytes 131104 | tf_op jit(solution)/shard_map/ppermute | solution.py:54
  371.9 19.7 %custom-call.32 = f32[2,128,128]{1,2,0:T(8,128)S(1)} custom-call(f32[2,128,128]{2,1,0:T(8,128)S(1)} %get-tuple-element.143), custom_call_target="InvertDiagBlocksLowerTriangular" | custom-call | tf_op jit(solution)/shard_map/triangular_solve/custom-call.0 | solution.py:15
  (204 shorter events, 168.1 us)
Async XLA Ops:
  28.4 4.4 %collective-permute-start = (f32[256,256]{1,0:T(8,128)S(1)}, f32[256,256]{1,0:T(8,128)S(1)}, u32[]{:S(2)}, u32[]{:S(2)}) collective-permute-start(f32[256,256]{1,0:T(8,128)S(1)} %bitcast.184), channel_id=1, source_target_pairs={{0,4},{4,0},{1,5},{5,1},{2,6},{6,2},{3,7},{7,3},{8,12},{12,8},{9,1... | collective-permute-start | bytes 786440 | tf_op jit(solution)/shard_map/ppermute | solution.py:54
  31.9 7.9 %collective-permute-start.4 = (f32[256,256]{0,1:T(8,128)S(1)}, f32[256,256]{0,1:T(8,128)S(1)}, u32[]{:S(2)}, u32[]{:S(2)}) collective-permute-start(f32[256,256]{0,1:T(8,128)S(1)} %fusion.88), channel_id=1, source_target_pairs={{0,1},{1,0},{2,3},{3,2},{4,5},{5,4},{6,7},{7,6},{8,9},{9,8},{10,11... | collective-permute-start | bytes 786440 | tf_op jit(solution)/shard_map/ppermute | solution.py:54
  32.2 14.9 %collective-permute-start.3 = (f32[256,256]{0,1:T(8,128)S(1)}, f32[256,256]{0,1:T(8,128)S(1)}, u32[]{:S(2)}, u32[]{:S(2)}) collective-permute-start(f32[256,256]{0,1:T(8,128)S(1)} %fusion.87), channel_id=1, source_target_pairs={{0,4},{4,0},{1,5},{5,1},{2,6},{6,2},{3,7},{7,3},{8,12},{12,8},{9,1... | collective-permute-start | bytes 786440 | tf_op jit(solution)/shard_map/ppermute | solution.py:54
  32.8 12.6 %collective-permute-start.1 = (f32[256,256]{1,0:T(8,128)S(1)}, f32[256,256]{1,0:T(8,128)S(1)}, u32[]{:S(2)}, u32[]{:S(2)}) collective-permute-start(f32[256,256]{1,0:T(8,128)S(1)} %bitcast_add_fusion.3), channel_id=1, source_target_pairs={{0,1},{1,0},{2,3},{3,2},{4,5},{5,4},{6,7},{7,6},{8,9},{9,8},{10,11... | collective-permute-start | bytes 786440 | tf_op jit(solution)/shard_map/ppermute | solution.py:54
  39.9 11.7 %collective-permute-start.5 = (f32[256,256]{0,1:T(8,128)S(1)}, f32[256,256]{0,1:T(8,128)S(1)}, u32[]{:S(2)}, u32[]{:S(2)}) collective-permute-start(f32[256,256]{0,1:T(8,128)S(1)} %add.166), channel_id=1, source_target_pairs={{0,2},{1,3},{2,0},{3,1},{4,6},{5,7},{6,4},{7,5},{8,10},{9,11},{10,... | collective-permute-start | bytes 786440 | tf_op jit(solution)/shard_map/ppermute | solution.py:54
  45.5 70.8 %collective-permute-start.2 = (f32[256,256]{1,0:T(8,128)S(1)}, f32[256,256]{1,0:T(8,128)S(1)}, u32[]{:S(2)}, u32[]{:S(2)}) collective-permute-start(f32[256,256]{1,0:T(8,128)S(1)} %add.163), channel_id=1, source_target_pairs={{0,2},{1,3},{2,0},{3,1},{4,6},{5,7},{6,4},{7,5},{8,10},{9,11},{10,... | collective-permute-start | bytes 786440 | tf_op jit(solution)/shard_map/ppermute | solution.py:54
  117.7 7.0 %collective-permute-start.6 = (f32[256,256]{0,1:T(8,128)S(1)}, f32[256,256]{0,1:T(8,128)S(1)}, u32[]{:S(2)}, u32[]{:S(2)}) collective-permute-start(f32[256,256]{0,1:T(8,128)S(1)} %fusion.89), channel_id=1, source_target_pairs={{0,8},{8,0},{16,24},{24,16},{32,40},{40,32},{48,56},{56,48},{64,72... | collective-permute-start | bytes 786440 | tf_op jit(solution)/shard_map/ppermute | solution.py:54
  124.7 14.4 %collective-permute-start.7 = (f32[256,256]{0,1:T(8,128)S(1)}, f32[256,256]{0,1:T(8,128)S(1)}, u32[]{:S(2)}, u32[]{:S(2)}) collective-permute-start(f32[256,256]{0,1:T(8,128)S(1)} %add.169), channel_id=1, source_target_pairs={{0,16},{8,24},{16,0},{24,8},{32,48},{40,56},{48,32},{56,40},{64,80... | collective-permute-start | bytes 786440 | tf_op jit(solution)/shard_map/ppermute | solution.py:54
  139.2 15.3 %collective-permute-start.8 = (f32[256,256]{0,1:T(8,128)S(1)}, f32[256,256]{0,1:T(8,128)S(1)}, u32[]{:S(2)}, u32[]{:S(2)}) collective-permute-start(f32[256,256]{0,1:T(8,128)S(1)} %add.170), channel_id=1, source_target_pairs={{0,32},{8,40},{16,48},{24,56},{32,0},{40,8},{48,16},{56,24},{64,96... | collective-permute-start | bytes 786440 | tf_op jit(solution)/shard_map/ppermute | solution.py:54
  154.5 5.3 %collective-permute-start.9 = (f32[256,256]{0,1:T(8,128)S(1)}, f32[256,256]{0,1:T(8,128)S(1)}, u32[]{:S(2)}, u32[]{:S(2)}) collective-permute-start(f32[256,256]{0,1:T(8,128)S(1)} %add.171), channel_id=1, source_target_pairs={{0,64},{8,72},{16,80},{24,88},{32,96},{40,104},{48,112},{56,120},{... | collective-permute-start | bytes 786440 | tf_op jit(solution)/shard_map/ppermute | solution.py:54
  159.8 9.3 %collective-permute-start.10 = (f32[256,256]{0,1:T(8,128)S(1)}, f32[256,256]{0,1:T(8,128)S(1)}, u32[]{:S(2)}, u32[]{:S(2)}) collective-permute-start(f32[256,256]{0,1:T(8,128)S(1)} %add.172), channel_id=1, source_target_pairs={{0,128},{8,136},{16,144},{24,152},{32,160},{40,168},{48,176},{56,1... | collective-permute-start | bytes 786440 | tf_op jit(solution)/shard_map/ppermute | solution.py:54
  217.8 3.9 collective-permute-start.11
  221.8 7.2 %collective-permute-start.12 = (f32[128,256]{1,0:T(8,128)S(1)}, f32[128,256]{1,0:T(8,128)S(1)}, u32[]{:S(2)}, u32[]{:S(2)}) collective-permute-start(f32[128,256]{1,0:T(8,128)S(1)} %add.177), channel_id=1, source_target_pairs={{0,16},{8,24},{16,0},{24,8},{32,48},{40,56},{48,32},{56,40},{64,80... | collective-permute-start | bytes 393224 | tf_op jit(solution)/shard_map/ppermute | solution.py:54
  229.0 9.2 %collective-permute-start.13 = (f32[128,256]{1,0:T(8,128)S(1)}, f32[128,256]{1,0:T(8,128)S(1)}, u32[]{:S(2)}, u32[]{:S(2)}) collective-permute-start(f32[128,256]{1,0:T(8,128)S(1)} %add.178), channel_id=1, source_target_pairs={{0,32},{8,40},{16,48},{24,56},{32,0},{40,8},{48,16},{56,24},{64,96... | collective-permute-start | bytes 393224 | tf_op jit(solution)/shard_map/ppermute | solution.py:54
  238.2 25.5 %collective-permute-start.14 = (f32[128,256]{1,0:T(8,128)S(1)}, f32[128,256]{1,0:T(8,128)S(1)}, u32[]{:S(2)}, u32[]{:S(2)}) collective-permute-start(f32[128,256]{1,0:T(8,128)S(1)} %add.179), channel_id=1, source_target_pairs={{0,64},{8,72},{16,80},{24,88},{32,96},{40,104},{48,112},{56,120},{... | collective-permute-start | bytes 393224 | tf_op jit(solution)/shard_map/ppermute | solution.py:54
  263.7 5.4 %collective-permute-start.15 = (f32[128,256]{1,0:T(8,128)S(1)}, f32[128,256]{1,0:T(8,128)S(1)}, u32[]{:S(2)}, u32[]{:S(2)}) collective-permute-start(f32[128,256]{1,0:T(8,128)S(1)} %add.180), channel_id=1, source_target_pairs={{0,128},{8,136},{16,144},{24,152},{32,160},{40,168},{48,176},{56,1... | collective-permute-start | bytes 393224 | tf_op jit(solution)/shard_map/ppermute | solution.py:54
  273.0 5.4 %collective-permute-start.17 = (f32[128,256]{1,0:T(8,128)S(1)}, f32[128,256]{1,0:T(8,128)S(1)}, u32[]{:S(2)}, u32[]{:S(2)}) collective-permute-start(f32[128,256]{1,0:T(8,128)S(1)} %add.182), channel_id=1, source_target_pairs={{0,2},{1,3},{2,0},{3,1},{4,6},{5,7},{6,4},{7,5},{8,10},{9,11},{10,... | collective-permute-start | bytes 393224 | tf_op jit(solution)/shard_map/ppermute | solution.py:54
  279.6 23.1 %collective-permute-start.18 = (f32[256,256]{0,1:T(8,128)S(1)}, f32[256,256]{0,1:T(8,128)S(1)}, u32[]{:S(2)}, u32[]{:S(2)}) collective-permute-start(f32[256,256]{0,1:T(8,128)S(1)} %fusion.90), channel_id=1, source_target_pairs={{0,4},{4,0},{1,5},{5,1},{2,6},{6,2},{3,7},{7,3},{8,12},{12,8},{9,1... | collective-permute-start | bytes 786440 | tf_op jit(solution)/shard_map/ppermute | solution.py:54
  350.4 5.1 %collective-permute-start.19 = (f32[128,256]{1,0:T(8,128)S(1)}, f32[128,256]{1,0:T(8,128)S(1)}, u32[]{:S(2)}, u32[]{:S(2)}) collective-permute-start(f32[128,256]{1,0:T(8,128)S(1)} %get-tuple-element.77), channel_id=1, source_target_pairs={{0,8},{8,0},{16,24},{24,16},{32,40},{40,32},{48,56},{56,48},{64,72... | collective-permute-start | bytes 393224 | tf_op jit(solution)/shard_map/ppermute | solution.py:54
  355.5 9.2 %collective-permute-start.20 = (f32[128,256]{1,0:T(8,128)S(1)}, f32[128,256]{1,0:T(8,128)S(1)}, u32[]{:S(2)}, u32[]{:S(2)}) collective-permute-start(f32[128,256]{1,0:T(8,128)S(1)} %add.187), channel_id=1, source_target_pairs={{0,16},{8,24},{16,0},{24,8},{32,48},{40,56},{48,32},{56,40},{64,80... | collective-permute-start | bytes 393224 | tf_op jit(solution)/shard_map/ppermute | solution.py:54
  364.7 26.8 %collective-permute-start.21 = (f32[128,256]{1,0:T(8,128)S(1)}, f32[128,256]{1,0:T(8,128)S(1)}, u32[]{:S(2)}, u32[]{:S(2)}) collective-permute-start(f32[128,256]{1,0:T(8,128)S(1)} %add.188), channel_id=1, source_target_pairs={{0,32},{8,40},{16,48},{24,56},{32,0},{40,8},{48,16},{56,24},{64,96... | collective-permute-start | bytes 393224 | tf_op jit(solution)/shard_map/ppermute | solution.py:54
  395.5 5.4 %collective-permute-start.23 = (f32[128,256]{1,0:T(8,128)S(1)}, f32[128,256]{1,0:T(8,128)S(1)}, u32[]{:S(2)}, u32[]{:S(2)}) collective-permute-start(f32[128,256]{1,0:T(8,128)S(1)} %add.190), channel_id=1, source_target_pairs={{0,128},{8,136},{16,144},{24,152},{32,160},{40,168},{48,176},{56,1... | collective-permute-start | bytes 393224 | tf_op jit(solution)/shard_map/ppermute | solution.py:54
  400.9 4.8 %collective-permute-start.24 = (f32[128,256]{1,0:T(8,128)S(1)}, f32[128,256]{1,0:T(8,128)S(1)}, u32[]{:S(2)}, u32[]{:S(2)}) collective-permute-start(f32[128,256]{1,0:T(8,128)S(1)} %add.191), channel_id=1, source_target_pairs={{0,4},{4,0},{1,5},{5,1},{2,6},{6,2},{3,7},{7,3},{8,12},{12,8},{9,1... | collective-permute-start | bytes 393224 | tf_op jit(solution)/shard_map/ppermute | solution.py:54
  409.0 3.9 collective-permute-start.26
  (8 other events, 161.3 us)

commit v4 on v3

--- a/solution.py
+++ b/solution.py
@@ -72,10 +72,15 @@
     inverse_neuron = normal_inverse(start_time * start_trial)
     kr_tk = khatri_rao(time_factor, trial_factor)
     neuron_total = neuron_rows * lax.axis_size("neuron")
-    kr_masked = kr_tk[None, :, :, :] * block_mask[:, None, :, None]
+    kr_masked = (kr_tk[None, :, :, :] * block_mask[:, None, :, None]).reshape(
+        block_count, time_rows * trial_rows, rank_size
+    )
     block_sums = tree_sum(
         jnp.einsum(
-            "bitk,btkr->bir", blocks, kr_masked, preferred_element_type=jnp.float32
+            "bix,bxr->bir",
+            tensor.reshape(block_count, block_rows, time_rows * trial_rows),
+            kr_masked,
+            preferred_element_type=jnp.float32,
         ).reshape(neuron_rows, rank_size),
         ("tm", "trial"),
     )
@@ -112,17 +117,22 @@
 
     def trial_add_block(running, inputs):
         tensor_piece, mask_row, rows_a = inputs
-        kr_it = khatri_rao(rows_a, time_local)
-        block_part = jnp.einsum(
-            "itk,itr->kr", tensor_piece, kr_it, preferred_element_type=jnp.float32
+        kr_ti = (
+            rows_a.T.astype(jnp.float32)[:, :, None] * time_local.T.astype(jnp.float32)[:, None, :]
+        ).astype(jnp.bfloat16)
+        block_part = jnp.dot(
+            kr_ti.reshape(rank_size, block_rows * time_rows),
+            tensor_piece.reshape(block_rows * time_rows, trial_rows),
+            preferred_element_type=jnp.float32,
         )
-        return (running + block_part * mask_row.astype(jnp.float32)[:, None], None)
+        return (running + block_part * mask_row.astype(jnp.float32)[None, :], None)
 
     running, unused = lax.scan(
         trial_add_block,
-        jnp.zeros((trial_rows, rank_size), jnp.float32),
+        jnp.zeros((rank_size, trial_rows), jnp.float32),
         (blocks, block_mask, neuron_blocks),
     )
+    running = running.T
     running, gram_time = lax.optimization_barrier((running, gram_time))
     quarter_sums = tree_sum(running, ("neuron", "tm"))
     inverse_trial = normal_inverse(gram_neuron * gram_time)

time: 422 us -> 449 us (1.064)
  matrix products: 31.5 us -> 48.1 us
  other arithmetic: 173 us -> 184 us
    dot_general x3, matrix products: 15.3 us -> 31.9 us  [the longest x2 19.3 us: trial_add_block(): jnp.dot(kr_ti.reshape(rank_size, block_rows * time_rows), tensor_piece.re...]
    convert_element_type x2 -> x6, other arithmetic: 0.02 us -> 14.3 us  [the longest x2 14.2 us: trial_add_block(): kr_ti = (rows_a.T.astype(jnp.float32)[:, :, None] * time_local.T.astype(j...]
    unnamed x13 -> x16, local copies, waits for them, and re-layouts: 12.8 us -> 0.91 us
    dynamic_slice x0 -> x2, local copies, waits for them, and re-layouts: none -> 9.49 us  [on_device(): lax.scan(time_add_block, jnp.zeros((time_rows, rank_size), jnp.float32),...]
  transfers between devices with their start and end apart: 27 -> 27, of which waited for: 22 -> 23; matrix products, arithmetic and copies ran while one was open for 31% -> 26% of each run, Pallas kernels for 0% -> 0%
where the time goes in v4:
time: 449 us; the launch traced here: 442 us
  other arithmetic  184 us (41%)
  waiting for transfers between devices  90.4 us (20%)
  starting transfers between devices  61.7 us (14%)
  local copies, waits for them, and re-layouts  49.4 us (11%)
  matrix products  48.1 us (11%)
  between operations  7.84 us (2%)
    another operation x20, other arithmetic, normal_inverse(): lower_factor = jnp.linalg.cholesky(scaled)  103 us
    ppermute x27, waiting for transfers between devices, tree_sum(): values = values + lax.ppermute(values, axis, pairs)  90.4 us
    ppermute x27, starting transfers between devices, tree_sum(): values = values + lax.ppermute(values, axis, pairs)  61.7 us
    another operation x7, other arithmetic, normal_inverse(): lax.linalg.triangular_solve(lower_factor, identity, left_side=True, lower...  59.3 us
    dot_general x2, matrix products, trial_add_block(): jnp.dot(kr_ti.reshape(rank_size, block_rows * time_rows), tensor_piece.re...  19.3 us
    convert_element_type x2, other arithmetic, trial_add_block(): kr_ti = (rows_a.T.astype(jnp.float32)[:, :, None] * time_local.T.astype(j...  14.2 us
    reshape x1, local copies, waits for them, and re-layouts, on_device(): tensor.reshape(block_count, block_rows, time_rows * trial_rows)  13.4 us
    dot_general x1, matrix products, on_device(): jnp.einsum('bix,bxr->bir', tensor.reshape(block_count, block_rows, time_r...  12.5 us
  transfers between devices with their start and end apart: 27, of which 23 were waited for; matrix products, arithmetic and copies ran while one was open for 26% of the time, Pallas kernels for 0%

profile of v4, /device:TPU:1, one launch (start us, length us, event | category | flops | bytes accessed | tf_op | source)
XLA Modules:
  0.0 442.1 jit_solution(5369004914115524671)
XLA Ops:
  0.7 13.4 %reshape.103 = bf16[2,128,16384]{2,1,0:T(8,128)(2,1)} reshape(bf16[256,128,128]{2,1,0:T(8,128)(2,1)} %param.12) | data formatting | bytes 16777216 | tf_op jit(solution)/shard_map/reshape | solution.py:81
  18.0 12.5 %fusion.31 = f32[2,256,128]{1,2,0:T(8,128)S(1)} fusion(bf16[2,128,16384]{2,1,0:T(8,128)(2,1)S(1)} %copy-done, bf16[2,16384]{1,0:T(2,128)(2,1)S(1)} %bitcast.196, bf16[16384,256]{1,0:T(8,128)(2,1)S(1)} %bitcast.191), kind=kOutput, calls=%fused_computation.37 | convolution fusion | flops 2181038080 | bytes 17104896 | tf_op jit(solution)/shard_map/bix,bxr->bir/dot_general | solution.py:79
  57.6 11.7 %cholesky.172 = f32[128,128]{1,0:T(8,128)S(1)} custom-call(f32[128,128]{1,0:T(8,128)S(1)} %cholesky.270), custom_call_target="Cholesky" | custom-call | tf_op jit(solution)/shard_map/jit(cholesky)/cholesky | solution.py:14
  69.4 9.8 %custom-call.27 = f32[1,128,128]{1,2,0:T(8,128)S(1)} custom-call(f32[1,128,128]{2,1,0:T(8,128)S(1)} %get-tuple-element.241), custom_call_target="InvertDiagBlocksLowerTriangular" | custom-call | tf_op jit(solution)/shard_map/jit(cholesky)/cholesky | solution.py:14
  79.7 11.7 %cholesky.189 = f32[128,128]{1,0:T(8,128)S(1)} custom-call(f32[128,128]{1,0:T(8,128)S(1)} %convolution_subtract_fusion.5), custom_call_target="Cholesky" | custom-call | tf_op jit(solution)/shard_map/jit(cholesky)/cholesky | solution.py:14
  97.5 19.9 %custom-call.28 = f32[2,128,128]{1,2,0:T(8,128)S(1)} custom-call(f32[2,128,128]{2,1,0:T(8,128)S(1)} %get-tuple-element.141), custom_call_target="InvertDiagBlocksLowerTriangular" | custom-call | tf_op jit(solution)/shard_map/triangular_solve/custom-call.0 | solution.py:15
  129.9 11.4 %collective-permute-done.7 = f32[256,256]{0,1:T(8,128)S(1)} collective-permute-done((f32[256,256]{0,1:T(8,128)S(1)}, f32[256,256]{0,1:T(8,128)S(1)}, u32[]{:S(2)}, u32[]{:S(2)}) %collective-permute-start.7) | collective-permute-done | bytes 262176 | tf_op jit(solution)/shard_map/ppermute | solution.py:54
  147.9 8.7 %collective-permute-done.8 = f32[256,256]{0,1:T(8,128)S(1)} collective-permute-done((f32[256,256]{0,1:T(8,128)S(1)}, f32[256,256]{0,1:T(8,128)S(1)}, u32[]{:S(2)}, u32[]{:S(2)}) %collective-permute-start.8) | collective-permute-done | bytes 262176 | tf_op jit(solution)/shard_map/ppermute | solution.py:54
  173.9 8.1 %while.28 = (s32[]{:T(128)}, f32[128,256]{1,0:T(8,128)S(1)}, bf16[2,128,128,128]{3,2,1,0:T(8,128)(2,1)}, bf16[2,128,256]{2,1,0:T(8,128)(2,1)S(1)}, bf16[128,256]...) while((s32[]{:T(128)}, f32[128,256]{1,0:T(8,128)S(1)}, ...), condition=%wide.region_6.9_spmd.clone, body=%wide.region_5.8_spmd.clone.sunk | while | flops 1086455808 | bytes 5112691 | solution.py:105
  186.4 11.7 %cholesky.206 = f32[128,128]{1,0:T(8,128)S(1)} custom-call(f32[128,128]{1,0:T(8,128)S(1)} %cholesky.273), custom_call_target="Cholesky" | custom-call | tf_op jit(solution)/shard_map/jit(cholesky)/cholesky | solution.py:14
  198.2 9.8 %custom-call.29 = f32[1,128,128]{1,2,0:T(8,128)S(1)} custom-call(f32[1,128,128]{2,1,0:T(8,128)S(1)} %get-tuple-element.237), custom_call_target="InvertDiagBlocksLowerTriangular" | custom-call | tf_op jit(solution)/shard_map/jit(cholesky)/cholesky | solution.py:14
  208.5 11.7 %cholesky.223 = f32[128,128]{1,0:T(8,128)S(1)} custom-call(f32[128,128]{1,0:T(8,128)S(1)} %convolution_subtract_fusion.4), custom_call_target="Cholesky" | custom-call | tf_op jit(solution)/shard_map/jit(cholesky)/cholesky | solution.py:14
  246.1 19.7 %custom-call.30 = f32[2,128,128]{1,2,0:T(8,128)S(1)} custom-call(f32[2,128,128]{2,1,0:T(8,128)S(1)} %get-tuple-element.142), custom_call_target="InvertDiagBlocksLowerTriangular" | custom-call | tf_op jit(solution)/shard_map/triangular_solve/custom-call.0 | solution.py:15
  281.7 11.3 %collective-permute-start.18 = (f32[256,256]{0,1:T(8,128)S(1)}, f32[256,256]{0,1:T(8,128)S(1)}, u32[]{:S(2)}, u32[]{:S(2)}) collective-permute-start(f32[256,256]{0,1:T(8,128)S(1)} %fusion.84), channel_id=1, source_target_pairs={{0,4},{4,0},{1,5},{5,1},{2,6},{6,2},{3,7},{7,3},{8,12},{12,8},{9,1... | collective-permute-start | bytes 786440 | tf_op jit(solution)/shard_map/ppermute | solution.py:54
  296.7 43.6 %while.29 = (s32[]{:T(128)}, f32[256,128]{1,0:T(8,128)S(1)}, bf16[2,128,256]{2,1,0:T(8,128)(2,1)S(1)}, bf16[128,256]{1,0:T(8,128)(2,1)S(1)}, bf16[2,128,128,128]...) while((s32[]{:T(128)}, f32[256,128]{1,0:T(8,128)S(1)}, ...), condition=%wide.region_9.12_spmd.clone, body=%wide.region_8.11_spmd.clone.sunk | while | flops 1082294400 | bytes 30803312 | solution.py:130
  301.7 7.1 %multiply_convert_fusion.4 = bf16[256,128,128]{2,1,0:T(8,128)(2,1)} fusion(f32[256,128]{1,0:T(8,128)S(1)} %copy.63, f32[256,128]{1,0:T(8,128)S(1)} %copy.64), kind=kLoop, calls=%fused_computation.25.clone.1 | loop fusion | flops 8388608 | bytes 8650752 | tf_op jit(solution)/shard_map/while/body/eval_jaxpr/convert_element_type | solution.py:122
  308.9 9.7 %fusion.128 = f32[256,128]{1,0:T(8,128)S(1)} fusion(bf16[16384,128]{1,0:T(8,128)(2,1)} %bitcast.189, bf16[32,8,128,128]{3,2,1,0:T(8,128)(2,1)} %bitcast.188, f32[256,128]{1,0:T(8,128)S(1)} %get-tuple-element.478, f32[128]{0:T(128)S(1)} %fusion.127, pred[]{:T(512)S(6)} %compare.42), kind=kOutput, calls=%fused_computation.30.clone.1 | convolution fusion | flops 1073840128 | bytes 12845569 | tf_op jit(solution)/shard_map/while/body/eval_jaxpr/dot_general | solution.py:123
  323.5 7.1 %multiply_convert_fusion.4 = bf16[256,128,128]{2,1,0:T(8,128)(2,1)} fusion(f32[256,128]{1,0:T(8,128)S(1)} %copy.63, f32[256,128]{1,0:T(8,128)S(1)} %copy.64), kind=kLoop, calls=%fused_computation.25.clone.1 | loop fusion | flops 8388608 | bytes 8650752 | tf_op jit(solution)/shard_map/while/body/eval_jaxpr/convert_element_type | solution.py:122
  330.7 9.7 %fusion.128 = f32[256,128]{1,0:T(8,128)S(1)} fusion(bf16[16384,128]{1,0:T(8,128)(2,1)} %bitcast.189, bf16[32,8,128,128]{3,2,1,0:T(8,128)(2,1)} %bitcast.188, f32[256,128]{1,0:T(8,128)S(1)} %get-tuple-element.478, f32[128]{0:T(128)S(1)} %fusion.127, pred[]{:T(512)S(6)} %compare.42), kind=kOutput, calls=%fused_computation.30.clone.1 | convolution fusion | flops 1073840128 | bytes 12845569 | tf_op jit(solution)/shard_map/while/body/eval_jaxpr/dot_general | solution.py:123
  344.5 11.7 %cholesky.240 = f32[128,128]{1,0:T(8,128)S(1)} custom-call(f32[128,128]{1,0:T(8,128)S(1)} %cholesky.276), custom_call_target="Cholesky" | custom-call | tf_op jit(solution)/shard_map/jit(cholesky)/cholesky | solution.py:14
  356.3 9.8 %custom-call.31 = f32[1,128,128]{1,2,0:T(8,128)S(1)} custom-call(f32[1,128,128]{2,1,0:T(8,128)S(1)} %get-tuple-element.233), custom_call_target="InvertDiagBlocksLowerTriangular" | custom-call | tf_op jit(solution)/shard_map/jit(cholesky)/cholesky | solution.py:14
  366.6 11.7 %cholesky.257 = f32[128,128]{1,0:T(8,128)S(1)} custom-call(f32[128,128]{1,0:T(8,128)S(1)} %convolution_subtract_fusion.3), custom_call_target="Cholesky" | custom-call | tf_op jit(solution)/shard_map/jit(cholesky)/cholesky | solution.py:14
  384.7 7.6 %collective-permute-done.20 = f32[128,256]{0,1:T(8,128)S(1)} collective-permute-done((f32[128,256]{0,1:T(8,128)S(1)}, f32[128,256]{0,1:T(8,128)S(1)}, u32[]{:S(2)}, u32[]{:S(2)}) %collective-permute-start.20) | collective-permute-done | bytes 131104 | tf_op jit(solution)/shard_map/ppermute | solution.py:54
  399.7 19.7 %custom-call.32 = f32[2,128,128]{1,2,0:T(8,128)S(1)} custom-call(f32[2,128,128]{2,1,0:T(8,128)S(1)} %get-tuple-element.143), custom_call_target="InvertDiagBlocksLowerTriangular" | custom-call | tf_op jit(solution)/shard_map/triangular_solve/custom-call.0 | solution.py:15
  (215 shorter events, 188.7 us)
Async XLA Ops:
  30.5 4.5 %collective-permute-start = (f32[256,256]{1,0:T(8,128)S(1)}, f32[256,256]{1,0:T(8,128)S(1)}, u32[]{:S(2)}, u32[]{:S(2)}) collective-permute-start(f32[256,256]{1,0:T(8,128)S(1)} %bitcast.193), channel_id=1, source_target_pairs={{0,4},{4,0},{1,5},{5,1},{2,6},{6,2},{3,7},{7,3},{8,12},{12,8},{9,1... | collective-permute-start | bytes 786440 | tf_op jit(solution)/shard_map/ppermute | solution.py:54
  34.0 7.9 %collective-permute-start.4 = (f32[256,256]{0,1:T(8,128)S(1)}, f32[256,256]{0,1:T(8,128)S(1)}, u32[]{:S(2)}, u32[]{:S(2)}) collective-permute-start(f32[256,256]{0,1:T(8,128)S(1)} %fusion.82), channel_id=1, source_target_pairs={{0,1},{1,0},{2,3},{3,2},{4,5},{5,4},{6,7},{7,6},{8,9},{9,8},{10,11... | collective-permute-start | bytes 786440 | tf_op jit(solution)/shard_map/ppermute | solution.py:54
  34.3 14.6 %collective-permute-start.3 = (f32[256,256]{0,1:T(8,128)S(1)}, f32[256,256]{0,1:T(8,128)S(1)}, u32[]{:S(2)}, u32[]{:S(2)}) collective-permute-start(f32[256,256]{0,1:T(8,128)S(1)} %fusion.81), channel_id=1, source_target_pairs={{0,4},{4,0},{1,5},{5,1},{2,6},{6,2},{3,7},{7,3},{8,12},{12,8},{9,1... | collective-permute-start | bytes 786440 | tf_op jit(solution)/shard_map/ppermute | solution.py:54
  35.0 12.6 %collective-permute-start.1 = (f32[256,256]{1,0:T(8,128)S(1)}, f32[256,256]{1,0:T(8,128)S(1)}, u32[]{:S(2)}, u32[]{:S(2)}) collective-permute-start(f32[256,256]{1,0:T(8,128)S(1)} %bitcast_add_fusion.3), channel_id=1, source_target_pairs={{0,1},{1,0},{2,3},{3,2},{4,5},{5,4},{6,7},{7,6},{8,9},{9,8},{10,11... | collective-permute-start | bytes 786440 | tf_op jit(solution)/shard_map/ppermute | solution.py:54
  42.0 11.7 %collective-permute-start.5 = (f32[256,256]{0,1:T(8,128)S(1)}, f32[256,256]{0,1:T(8,128)S(1)}, u32[]{:S(2)}, u32[]{:S(2)}) collective-permute-start(f32[256,256]{0,1:T(8,128)S(1)} %add.166), channel_id=1, source_target_pairs={{0,2},{1,3},{2,0},{3,1},{4,6},{5,7},{6,4},{7,5},{8,10},{9,11},{10,... | collective-permute-start | bytes 786440 | tf_op jit(solution)/shard_map/ppermute | solution.py:54
  47.6 70.8 %collective-permute-start.2 = (f32[256,256]{1,0:T(8,128)S(1)}, f32[256,256]{1,0:T(8,128)S(1)}, u32[]{:S(2)}, u32[]{:S(2)}) collective-permute-start(f32[256,256]{1,0:T(8,128)S(1)} %add.163), channel_id=1, source_target_pairs={{0,2},{1,3},{2,0},{3,1},{4,6},{5,7},{6,4},{7,5},{8,10},{9,11},{10,... | collective-permute-start | bytes 786440 | tf_op jit(solution)/shard_map/ppermute | solution.py:54
  119.9 7.0 %collective-permute-start.6 = (f32[256,256]{0,1:T(8,128)S(1)}, f32[256,256]{0,1:T(8,128)S(1)}, u32[]{:S(2)}, u32[]{:S(2)}) collective-permute-start(f32[256,256]{0,1:T(8,128)S(1)} %fusion.83), channel_id=1, source_target_pairs={{0,8},{8,0},{16,24},{24,16},{32,40},{40,32},{48,56},{56,48},{64,72... | collective-permute-start | bytes 786440 | tf_op jit(solution)/shard_map/ppermute | solution.py:54
  126.9 14.5 %collective-permute-start.7 = (f32[256,256]{0,1:T(8,128)S(1)}, f32[256,256]{0,1:T(8,128)S(1)}, u32[]{:S(2)}, u32[]{:S(2)}) collective-permute-start(f32[256,256]{0,1:T(8,128)S(1)} %add.169), channel_id=1, source_target_pairs={{0,16},{8,24},{16,0},{24,8},{32,48},{40,56},{48,32},{56,40},{64,80... | collective-permute-start | bytes 786440 | tf_op jit(solution)/shard_map/ppermute | solution.py:54
  141.4 15.2 %collective-permute-start.8 = (f32[256,256]{0,1:T(8,128)S(1)}, f32[256,256]{0,1:T(8,128)S(1)}, u32[]{:S(2)}, u32[]{:S(2)}) collective-permute-start(f32[256,256]{0,1:T(8,128)S(1)} %add.170), channel_id=1, source_target_pairs={{0,32},{8,40},{16,48},{24,56},{32,0},{40,8},{48,16},{56,24},{64,96... | collective-permute-start | bytes 786440 | tf_op jit(solution)/shard_map/ppermute | solution.py:54
  156.6 5.3 %collective-permute-start.9 = (f32[256,256]{0,1:T(8,128)S(1)}, f32[256,256]{0,1:T(8,128)S(1)}, u32[]{:S(2)}, u32[]{:S(2)}) collective-permute-start(f32[256,256]{0,1:T(8,128)S(1)} %add.171), channel_id=1, source_target_pairs={{0,64},{8,72},{16,80},{24,88},{32,96},{40,104},{48,112},{56,120},{... | collective-permute-start | bytes 786440 | tf_op jit(solution)/shard_map/ppermute | solution.py:54
  162.0 9.3 %collective-permute-start.10 = (f32[256,256]{0,1:T(8,128)S(1)}, f32[256,256]{0,1:T(8,128)S(1)}, u32[]{:S(2)}, u32[]{:S(2)}) collective-permute-start(f32[256,256]{0,1:T(8,128)S(1)} %add.172), channel_id=1, source_target_pairs={{0,128},{8,136},{16,144},{24,152},{32,160},{40,168},{48,176},{56,1... | collective-permute-start | bytes 786440 | tf_op jit(solution)/shard_map/ppermute | solution.py:54
  224.1 7.2 %collective-permute-start.12 = (f32[128,256]{1,0:T(8,128)S(1)}, f32[128,256]{1,0:T(8,128)S(1)}, u32[]{:S(2)}, u32[]{:S(2)}) collective-permute-start(f32[128,256]{1,0:T(8,128)S(1)} %add.177), channel_id=1, source_target_pairs={{0,16},{8,24},{16,0},{24,8},{32,48},{40,56},{48,32},{56,40},{64,80... | collective-permute-start | bytes 393224 | tf_op jit(solution)/shard_map/ppermute | solution.py:54
  231.3 9.2 %collective-permute-start.13 = (f32[128,256]{1,0:T(8,128)S(1)}, f32[128,256]{1,0:T(8,128)S(1)}, u32[]{:S(2)}, u32[]{:S(2)}) collective-permute-start(f32[128,256]{1,0:T(8,128)S(1)} %add.178), channel_id=1, source_target_pairs={{0,32},{8,40},{16,48},{24,56},{32,0},{40,8},{48,16},{56,24},{64,96... | collective-permute-start | bytes 393224 | tf_op jit(solution)/shard_map/ppermute | solution.py:54
  240.5 25.3 %collective-permute-start.14 = (f32[128,256]{1,0:T(8,128)S(1)}, f32[128,256]{1,0:T(8,128)S(1)}, u32[]{:S(2)}, u32[]{:S(2)}) collective-permute-start(f32[128,256]{1,0:T(8,128)S(1)} %add.179), channel_id=1, source_target_pairs={{0,64},{8,72},{16,80},{24,88},{32,96},{40,104},{48,112},{56,120},{... | collective-permute-start | bytes 393224 | tf_op jit(solution)/shard_map/ppermute | solution.py:54
  265.8 5.4 %collective-permute-start.15 = (f32[128,256]{1,0:T(8,128)S(1)}, f32[128,256]{1,0:T(8,128)S(1)}, u32[]{:S(2)}, u32[]{:S(2)}) collective-permute-start(f32[128,256]{1,0:T(8,128)S(1)} %add.180), channel_id=1, source_target_pairs={{0,128},{8,136},{16,144},{24,152},{32,160},{40,168},{48,176},{56,1... | collective-permute-start | bytes 393224 | tf_op jit(solution)/shard_map/ppermute | solution.py:54
  275.2 5.4 %collective-permute-start.17 = (f32[128,256]{1,0:T(8,128)S(1)}, f32[128,256]{1,0:T(8,128)S(1)}, u32[]{:S(2)}, u32[]{:S(2)}) collective-permute-start(f32[128,256]{1,0:T(8,128)S(1)} %add.182), channel_id=1, source_target_pairs={{0,2},{1,3},{2,0},{3,1},{4,6},{5,7},{6,4},{7,5},{8,10},{9,11},{10,... | collective-permute-start | bytes 393224 | tf_op jit(solution)/shard_map/ppermute | solution.py:54
  281.7 12.5 %collective-permute-start.18 = (f32[256,256]{0,1:T(8,128)S(1)}, f32[256,256]{0,1:T(8,128)S(1)}, u32[]{:S(2)}, u32[]{:S(2)}) collective-permute-start(f32[256,256]{0,1:T(8,128)S(1)} %fusion.84), channel_id=1, source_target_pairs={{0,4},{4,0},{1,5},{5,1},{2,6},{6,2},{3,7},{7,3},{8,12},{12,8},{9,1... | collective-permute-start | bytes 786440 | tf_op jit(solution)/shard_map/ppermute | solution.py:54
  378.3 4.8 %collective-permute-start.19 = (f32[128,256]{0,1:T(8,128)S(1)}, f32[128,256]{0,1:T(8,128)S(1)}, u32[]{:S(2)}, u32[]{:S(2)}) collective-permute-start(f32[128,256]{0,1:T(8,128)S(1)} %bitcast.194), channel_id=1, source_target_pairs={{0,8},{8,0},{16,24},{24,16},{32,40},{40,32},{48,56},{56,48},{64,72... | collective-permute-start | bytes 393224 | tf_op jit(solution)/shard_map/ppermute | solution.py:54
  383.1 9.2 %collective-permute-start.20 = (f32[128,256]{0,1:T(8,128)S(1)}, f32[128,256]{0,1:T(8,128)S(1)}, u32[]{:S(2)}, u32[]{:S(2)}) collective-permute-start(f32[128,256]{0,1:T(8,128)S(1)} %add.187), channel_id=1, source_target_pairs={{0,16},{8,24},{16,0},{24,8},{32,48},{40,56},{48,32},{56,40},{64,80... | collective-permute-start | bytes 393224 | tf_op jit(solution)/shard_map/ppermute | solution.py:54
  392.3 27.1 %collective-permute-start.21 = (f32[128,256]{0,1:T(8,128)S(1)}, f32[128,256]{0,1:T(8,128)S(1)}, u32[]{:S(2)}, u32[]{:S(2)}) collective-permute-start(f32[128,256]{0,1:T(8,128)S(1)} %add.188), channel_id=1, source_target_pairs={{0,32},{8,40},{16,48},{24,56},{32,0},{40,8},{48,16},{56,24},{64,96... | collective-permute-start | bytes 393224 | tf_op jit(solution)/shard_map/ppermute | solution.py:54
  419.4 3.9 collective-permute-start.22
  423.3 5.4 %collective-permute-start.23 = (f32[128,256]{0,1:T(8,128)S(1)}, f32[128,256]{0,1:T(8,128)S(1)}, u32[]{:S(2)}, u32[]{:S(2)}) collective-permute-start(f32[128,256]{0,1:T(8,128)S(1)} %add.190), channel_id=1, source_target_pairs={{0,128},{8,136},{16,144},{24,152},{32,160},{40,168},{48,176},{56,1... | collective-permute-start | bytes 393224 | tf_op jit(solution)/shard_map/ppermute | solution.py:54
  428.7 5.0 %collective-permute-start.24 = (f32[128,256]{0,1:T(8,128)S(1)}, f32[128,256]{0,1:T(8,128)S(1)}, u32[]{:S(2)}, u32[]{:S(2)}) collective-permute-start(f32[128,256]{0,1:T(8,128)S(1)} %add.191), channel_id=1, source_target_pairs={{0,4},{4,0},{1,5},{5,1},{2,6},{6,2},{3,7},{7,3},{8,12},{12,8},{9,1... | collective-permute-start | bytes 393224 | tf_op jit(solution)/shard_map/ppermute | solution.py:54
  437.0 3.9 collective-permute-start.26
  (9 other events, 169.8 us)

commit v5 on v3

--- a/solution.py
+++ b/solution.py
@@ -56,6 +56,19 @@
     return values
 
 
+def tree_gather(piece, steps):
+    for axis, stride in steps:
+        pairs = [(i, i ^ stride) for i in range(lax.axis_size(axis))]
+        other = lax.ppermute(piece, axis, pairs)
+        upper = (lax.axis_index(axis) // stride) % 2 == 1
+        piece = jnp.where(
+            upper,
+            jnp.concatenate([other, piece], axis=0),
+            jnp.concatenate([piece, other], axis=0),
+        )
+    return piece
+
+
 def factor_gram(rows):
     return jnp.dot(rows.T, rows, preferred_element_type=jnp.float32)
 
@@ -80,10 +93,14 @@
         ("tm", "trial"),
     )
     raw_rows = apply_inverse(block_sums, inverse_neuron)
-    gram_sum = tree_sum(raw_gram(raw_rows), ("neuron",))
-    neuron_local, gram_neuron = rescale(raw_rows, gram_sum, neuron_total)
     own_rows = neuron_rows // (lax.axis_size("tm") * lax.axis_size("trial"))
     own_index = lax.axis_index("tm") * lax.axis_size("trial") + lax.axis_index("trial")
+    own_columns = lax.dynamic_slice_in_dim(raw_rows, own_index * own_rows, own_rows, axis=1)
+    gram_piece = tree_sum(
+        jnp.dot(own_columns.T, raw_rows, precision=lax.Precision.HIGHEST), ("neuron",)
+    )
+    gram_sum = tree_gather(gram_piece, (("trial", 1), ("trial", 2), ("tm", 1)))
+    neuron_local, gram_neuron = rescale(raw_rows, gram_sum, neuron_total)
     neuron_own = lax.dynamic_slice_in_dim(neuron_local, own_index * own_rows, own_rows, axis=0)
     neuron_blocks = neuron_local.reshape(block_count, block_rows, rank_size)
     time_total = time_rows * lax.axis_size("tm")

time: 422 us -> 420 us (level)
  waiting for transfers between devices: 89.4 us -> 75.9 us
  starting transfers between devices: 62.1 us -> 72.8 us
    ppermute x27, waiting for transfers between devices: 89.4 us -> 66.5 us  [tree_sum(): values = values + lax.ppermute(values, axis, pairs)]
    ppermute x0 -> x3, starting transfers between devices: none -> 10.1 us  [tree_gather(): other = lax.ppermute(piece, axis, pairs)]
    ppermute x0 -> x3, waiting for transfers between devices: none -> 9.45 us  [tree_gather(): other = lax.ppermute(piece, axis, pairs)]
  transfers between devices with their start and end apart: 27 -> 30, of which waited for: 22 -> 25; matrix products, arithmetic and copies ran while one was open for 31% -> 31% of each run, Pallas kernels for 0% -> 0%
where the time goes in v5:
time: 420 us; the launch traced here: 412 us
  other arithmetic  173 us (41%)
  waiting for transfers between devices  75.9 us (18%)
  starting transfers between devices  72.8 us (17%)
  local copies, waits for them, and re-layouts  50.3 us (12%)
  matrix products  31.6 us (8%)
  between operations  7.61 us (2%)
    another operation x20, other arithmetic, normal_inverse(): lower_factor = jnp.linalg.cholesky(scaled)  103 us
    ppermute x27, waiting for transfers between devices, tree_sum(): values = values + lax.ppermute(values, axis, pairs)  66.5 us
    ppermute x27, starting transfers between devices, tree_sum(): values = values + lax.ppermute(values, axis, pairs)  62.7 us
    another operation x7, other arithmetic, normal_inverse(): lax.linalg.triangular_solve(lower_factor, identity, left_side=True, lower...  59.3 us
    unnamed x13, local copies, waits for them, and re-layouts  12.8 us
    reshape x1, local copies, waits for them, and re-layouts, on_device(): blocks = tensor.reshape(block_count, block_rows, time_rows, trial_rows)  12.4 us
    another operation x22, local copies, waits for them, and re-layouts, normal_inverse(): lax.linalg.triangular_solve(lower_factor, identity, left_side=True, lower...  12.2 us
    ppermute x3, starting transfers between devices, tree_gather(): other = lax.ppermute(piece, axis, pairs)  10.1 us
  transfers between devices with their start and end apart: 30, of which 25 were waited for; matrix products, arithmetic and copies ran while one was open for 31% of the time, Pallas kernels for 0%

profile of v5, /device:TPU:1, one launch (start us, length us, event | category | flops | bytes accessed | tf_op | source)
XLA Modules:
  0.0 412.1 jit_solution(17079245477779815684)
XLA Ops:
  0.7 12.4 %copy.27 = bf16[2,128,128,128]{2,1,3,0:T(8,128)(2,1)} copy(bf16[2,128,128,128]{3,2,1,0:T(8,128)(2,1)} %bitcast.178) | data formatting | bytes 16777216 | tf_op jit(solution)/shard_map/reshape | solution.py:81
  13.4 6.7 %multiply_convert_fusion.9 = bf16[128,128,256]{2,0,1:T(8,128)(2,1)} fusion(f32[128,256]{1,0:T(8,128)S(1)} %convert_element_type.92, f32[128,256]{1,0:T(8,128)S(1)} %convert_element_type.91), kind=kLoop, calls=%fused_computation.41 | loop fusion | flops 8388608 | bytes 8650752 | tf_op jit(solution)/shard_map/convert_element_type | solution.py:30
  20.1 8.3 %fusion.37 = f32[2,256,128,1]{1,2,3,0:T(8,128)S(1)} fusion(bf16[2,128,128,128]{2,1,3,0:T(8,128)(2,1)} %copy.27, bf16[2,128]{1,0:T(2,128)(2,1)S(1)} %fusion.41, bf16[128,128,256]{2,0,1:T(8,128)(2,1)} %multiply_convert_fusion.9), kind=kOutput, calls=%fused_computation.39 | convolution fusion | flops 2181038080 | bytes 17039872 | tf_op jit(solution)/shard_map/bitk,btkr->bir/dot_general | solution.py:90
  34.1 5.6 %collective-permute-done.4 = f32[256,256]{0,1:T(8,128)S(1)} collective-permute-done((f32[256,256]{0,1:T(8,128)S(1)}, f32[256,256]{0,1:T(8,128)S(1)}, u32[]{:S(2)}, u32[]{:S(2)}) %collective-permute-start.4) | collective-permute-done | bytes 262176 | tf_op jit(solution)/shard_map/ppermute | solution.py:54
  55.5 11.7 %cholesky.172 = f32[128,128]{1,0:T(8,128)S(1)} custom-call(f32[128,128]{1,0:T(8,128)S(1)} %cholesky.270), custom_call_target="Cholesky" | custom-call | tf_op jit(solution)/shard_map/jit(cholesky)/cholesky | solution.py:14
  67.2 9.8 %custom-call.27 = f32[1,128,128]{1,2,0:T(8,128)S(1)} custom-call(f32[1,128,128]{2,1,0:T(8,128)S(1)} %get-tuple-element.241), custom_call_target="InvertDiagBlocksLowerTriangular" | custom-call | tf_op jit(solution)/shard_map/jit(cholesky)/cholesky | solution.py:14
  77.5 11.7 %cholesky.189 = f32[128,128]{1,0:T(8,128)S(1)} custom-call(f32[128,128]{1,0:T(8,128)S(1)} %convolution_subtract_fusion.5), custom_call_target="Cholesky" | custom-call | tf_op jit(solution)/shard_map/jit(cholesky)/cholesky | solution.py:14
  95.5 19.8 %custom-call.28 = f32[2,128,128]{1,2,0:T(8,128)S(1)} custom-call(f32[2,128,128]{2,1,0:T(8,128)S(1)} %get-tuple-element.141), custom_call_target="InvertDiagBlocksLowerTriangular" | custom-call | tf_op jit(solution)/shard_map/triangular_solve/custom-call.0 | solution.py:15
  129.3 5.8 %collective-permute-start.8 = (f32[32,256]{0,1:T(8,128)S(1)}, f32[32,256]{0,1:T(8,128)S(1)}, u32[]{:S(2)}, u32[]{:S(2)}) collective-permute-start(f32[32,256]{0,1:T(8,128)S(1)} %add.189), channel_id=1, source_target_pairs={{0,32},{8,40},{16,48},{24,56},{32,0},{40,8},{48,16},{56,24},{64,96... | collective-permute-start | bytes 98312 | tf_op jit(solution)/shard_map/ppermute | solution.py:54
  157.2 9.4 %collective-permute-start.13 = (f32[128,256]{0,1:T(8,128)S(1)}, f32[128,256]{0,1:T(8,128)S(1)}, u32[]{:S(2)}, u32[]{:S(2)}) collective-permute-start(f32[128,256]{0,1:T(8,128)S(1)} %maximum_select_fusion.2), channel_id=1, source_target_pairs={{0,4},{4,0},{1,5},{5,1},{2,6},{6,2},{3,7},{7,3},{8,12},{12,8},{9,1... | collective-permute-start | bytes 393224 | tf_op jit(solution)/shard_map/ppermute | solution.py:62
  170.3 8.1 %while.28 = (s32[]{:T(128)}, f32[128,256]{1,0:T(8,128)S(1)}, bf16[2,128,128,128]{3,2,1,0:T(8,128)(2,1)}, bf16[2,128,256]{2,1,0:T(8,128)(2,1)S(1)}, bf16[128,256]...) while((s32[]{:T(128)}, f32[128,256]{1,0:T(8,128)S(1)}, ...), condition=%wide.region_6.9_spmd.clone, body=%wide.region_5.8_spmd.clone.sunk | while | flops 1086455808 | bytes 5112691 | solution.py:117
  182.6 11.7 %cholesky.206 = f32[128,128]{1,0:T(8,128)S(1)} custom-call(f32[128,128]{1,0:T(8,128)S(1)} %cholesky.273), custom_call_target="Cholesky" | custom-call | tf_op jit(solution)/shard_map/jit(cholesky)/cholesky | solution.py:14
  194.3 9.8 %custom-call.29 = f32[1,128,128]{1,2,0:T(8,128)S(1)} custom-call(f32[1,128,128]{2,1,0:T(8,128)S(1)} %get-tuple-element.237), custom_call_target="InvertDiagBlocksLowerTriangular" | custom-call | tf_op jit(solution)/shard_map/jit(cholesky)/cholesky | solution.py:14
  204.6 11.7 %cholesky.223 = f32[128,128]{1,0:T(8,128)S(1)} custom-call(f32[128,128]{1,0:T(8,128)S(1)} %convolution_subtract_fusion.4), custom_call_target="Cholesky" | custom-call | tf_op jit(solution)/shard_map/jit(cholesky)/cholesky | solution.py:14
  229.7 5.3 %collective-permute-start.16 = (f32[128,256]{1,0:T(8,128)S(1)}, f32[128,256]{1,0:T(8,128)S(1)}, u32[]{:S(2)}, u32[]{:S(2)}) collective-permute-start(f32[128,256]{1,0:T(8,128)S(1)} %add.195), channel_id=1, source_target_pairs={{0,32},{8,40},{16,48},{24,56},{32,0},{40,8},{48,16},{56,24},{64,96... | collective-permute-start | bytes 393224 | tf_op jit(solution)/shard_map/ppermute | solution.py:54
  243.9 19.7 %custom-call.30 = f32[2,128,128]{1,2,0:T(8,128)S(1)} custom-call(f32[2,128,128]{2,1,0:T(8,128)S(1)} %get-tuple-element.142), custom_call_target="InvertDiagBlocksLowerTriangular" | custom-call | tf_op jit(solution)/shard_map/triangular_solve/custom-call.0 | solution.py:15
  279.7 8.5 %collective-permute-start.21 = (f32[256,256]{0,1:T(8,128)S(1)}, f32[256,256]{0,1:T(8,128)S(1)}, u32[]{:S(2)}, u32[]{:S(2)}) collective-permute-start(f32[256,256]{0,1:T(8,128)S(1)} %fusion.92), channel_id=1, source_target_pairs={{0,4},{4,0},{1,5},{5,1},{2,6},{6,2},{3,7},{7,3},{8,12},{12,8},{9,1... | collective-permute-start | bytes 786440 | tf_op jit(solution)/shard_map/ppermute | solution.py:54
  288.2 12.0 %copy.26 = bf16[256,128,128]{1,2,0:T(8,128)(2,1)} copy(bf16[256,128,128]{2,1,0:T(8,128)(2,1)} %bitcast.180) | data formatting | bytes 16777216 | tf_op args[0]
  302.8 7.2 %while.29 = (s32[]{:T(128)}, f32[128,256]{1,0:T(8,128)S(1)}, bf16[2,128,128,128]{2,3,1,0:T(8,128)(2,1)}, bf16[2,128,256]{2,1,0:T(8,128)(2,1)S(1)}, bf16[128,256]...) while((s32[]{:T(128)}, f32[128,256]{1,0:T(8,128)S(1)}, ...), condition=%wide.region_9.12_spmd.clone, body=%wide.region_8.11_spmd.clone.sunk | while | flops 1082294400 | bytes 5113203 | solution.py:138
  314.1 11.7 %cholesky.240 = f32[128,128]{1,0:T(8,128)S(1)} custom-call(f32[128,128]{1,0:T(8,128)S(1)} %cholesky.276), custom_call_target="Cholesky" | custom-call | tf_op jit(solution)/shard_map/jit(cholesky)/cholesky | solution.py:14
  325.9 9.8 %custom-call.31 = f32[1,128,128]{1,2,0:T(8,128)S(1)} custom-call(f32[1,128,128]{2,1,0:T(8,128)S(1)} %get-tuple-element.233), custom_call_target="InvertDiagBlocksLowerTriangular" | custom-call | tf_op jit(solution)/shard_map/jit(cholesky)/cholesky | solution.py:14
  336.2 11.7 %cholesky.257 = f32[128,128]{1,0:T(8,128)S(1)} custom-call(f32[128,128]{1,0:T(8,128)S(1)} %convolution_subtract_fusion.3), custom_call_target="Cholesky" | custom-call | tf_op jit(solution)/shard_map/jit(cholesky)/cholesky | solution.py:14
  355.7 5.8 %collective-permute-done.23 = f32[128,256]{1,0:T(8,128)S(1)} collective-permute-done((f32[128,256]{1,0:T(8,128)S(1)}, f32[128,256]{1,0:T(8,128)S(1)}, u32[]{:S(2)}, u32[]{:S(2)}) %collective-permute-start.23) | collective-permute-done | bytes 131104 | tf_op jit(solution)/shard_map/ppermute | solution.py:54
  370.2 19.7 %custom-call.32 = f32[2,128,128]{1,2,0:T(8,128)S(1)} custom-call(f32[2,128,128]{2,1,0:T(8,128)S(1)} %get-tuple-element.143), custom_call_target="InvertDiagBlocksLowerTriangular" | custom-call | tf_op jit(solution)/shard_map/triangular_solve/custom-call.0 | solution.py:15
  (213 shorter events, 177.6 us)
Async XLA Ops:
  28.3 4.5 %collective-permute-start = (f32[256,256]{1,0:T(8,128)S(1)}, f32[256,256]{1,0:T(8,128)S(1)}, u32[]{:S(2)}, u32[]{:S(2)}) collective-permute-start(f32[256,256]{1,0:T(8,128)S(1)} %bitcast.183), channel_id=1, source_target_pairs={{0,4},{4,0},{1,5},{5,1},{2,6},{6,2},{3,7},{7,3},{8,12},{12,8},{9,1... | collective-permute-start | bytes 786440 | tf_op jit(solution)/shard_map/ppermute | solution.py:54
  31.9 7.9 %collective-permute-start.4 = (f32[256,256]{0,1:T(8,128)S(1)}, f32[256,256]{0,1:T(8,128)S(1)}, u32[]{:S(2)}, u32[]{:S(2)}) collective-permute-start(f32[256,256]{0,1:T(8,128)S(1)} %fusion.91), channel_id=1, source_target_pairs={{0,1},{1,0},{2,3},{3,2},{4,5},{5,4},{6,7},{7,6},{8,9},{9,8},{10,11... | collective-permute-start | bytes 786440 | tf_op jit(solution)/shard_map/ppermute | solution.py:54
  32.2 14.9 %collective-permute-start.3 = (f32[256,256]{0,1:T(8,128)S(1)}, f32[256,256]{0,1:T(8,128)S(1)}, u32[]{:S(2)}, u32[]{:S(2)}) collective-permute-start(f32[256,256]{0,1:T(8,128)S(1)} %fusion.90), channel_id=1, source_target_pairs={{0,4},{4,0},{1,5},{5,1},{2,6},{6,2},{3,7},{7,3},{8,12},{12,8},{9,1... | collective-permute-start | bytes 786440 | tf_op jit(solution)/shard_map/ppermute | solution.py:54
  32.8 12.6 %collective-permute-start.1 = (f32[256,256]{1,0:T(8,128)S(1)}, f32[256,256]{1,0:T(8,128)S(1)}, u32[]{:S(2)}, u32[]{:S(2)}) collective-permute-start(f32[256,256]{1,0:T(8,128)S(1)} %bitcast_add_fusion.3), channel_id=1, source_target_pairs={{0,1},{1,0},{2,3},{3,2},{4,5},{5,4},{6,7},{7,6},{8,9},{9,8},{10,11... | collective-permute-start | bytes 786440 | tf_op jit(solution)/shard_map/ppermute | solution.py:54
  39.8 11.7 %collective-permute-start.5 = (f32[256,256]{0,1:T(8,128)S(1)}, f32[256,256]{0,1:T(8,128)S(1)}, u32[]{:S(2)}, u32[]{:S(2)}) collective-permute-start(f32[256,256]{0,1:T(8,128)S(1)} %add.180), channel_id=1, source_target_pairs={{0,2},{1,3},{2,0},{3,1},{4,6},{5,7},{6,4},{7,5},{8,10},{9,11},{10,... | collective-permute-start | bytes 786440 | tf_op jit(solution)/shard_map/ppermute | solution.py:54
  45.4 71.0 %collective-permute-start.2 = (f32[256,256]{1,0:T(8,128)S(1)}, f32[256,256]{1,0:T(8,128)S(1)}, u32[]{:S(2)}, u32[]{:S(2)}) collective-permute-start(f32[256,256]{1,0:T(8,128)S(1)} %add.177), channel_id=1, source_target_pairs={{0,2},{1,3},{2,0},{3,1},{4,6},{5,7},{6,4},{7,5},{8,10},{9,11},{10,... | collective-permute-start | bytes 786440 | tf_op jit(solution)/shard_map/ppermute | solution.py:54
  122.0 7.3 %collective-permute-start.7 = (f32[32,256]{0,1:T(8,128)S(1)}, f32[32,256]{0,1:T(8,128)S(1)}, u32[]{:S(2)}, u32[]{:S(2)}) collective-permute-start(f32[32,256]{0,1:T(8,128)S(1)} %add.188), channel_id=1, source_target_pairs={{0,16},{8,24},{16,0},{24,8},{32,48},{40,56},{48,32},{56,40},{64,80... | collective-permute-start | bytes 98312 | tf_op jit(solution)/shard_map/ppermute | solution.py:54
  129.3 8.3 %collective-permute-start.8 = (f32[32,256]{0,1:T(8,128)S(1)}, f32[32,256]{0,1:T(8,128)S(1)}, u32[]{:S(2)}, u32[]{:S(2)}) collective-permute-start(f32[32,256]{0,1:T(8,128)S(1)} %add.189), channel_id=1, source_target_pairs={{0,32},{8,40},{16,48},{24,56},{32,0},{40,8},{48,16},{56,24},{64,96... | collective-permute-start | bytes 98312 | tf_op jit(solution)/shard_map/ppermute | solution.py:54
  137.6 4.2 %collective-permute-start.9 = (f32[32,256]{0,1:T(8,128)S(1)}, f32[32,256]{0,1:T(8,128)S(1)}, u32[]{:S(2)}, u32[]{:S(2)}) collective-permute-start(f32[32,256]{0,1:T(8,128)S(1)} %add.190), channel_id=1, source_target_pairs={{0,64},{8,72},{16,80},{24,88},{32,96},{40,104},{48,112},{56,120},{... | collective-permute-start | bytes 98312 | tf_op jit(solution)/shard_map/ppermute | solution.py:54
  141.8 5.7 %collective-permute-start.10 = (f32[32,256]{0,1:T(8,128)S(1)}, f32[32,256]{0,1:T(8,128)S(1)}, u32[]{:S(2)}, u32[]{:S(2)}) collective-permute-start(f32[32,256]{0,1:T(8,128)S(1)} %add.191), channel_id=1, source_target_pairs={{0,128},{8,136},{16,144},{24,152},{32,160},{40,168},{48,176},{56,1... | collective-permute-start | bytes 98312 | tf_op jit(solution)/shard_map/ppermute | solution.py:54
  151.6 5.4 %collective-permute-start.12 = (f32[64,256]{0,1:T(8,128)S(1)}, f32[64,256]{0,1:T(8,128)S(1)}, u32[]{:S(2)}, u32[]{:S(2)}) collective-permute-start(f32[64,256]{0,1:T(8,128)S(1)} %maximum_select_fusion.1), channel_id=1, source_target_pairs={{0,2},{1,3},{2,0},{3,1},{4,6},{5,7},{6,4},{7,5},{8,10},{9,11},{10,... | collective-permute-start | bytes 196616 | tf_op jit(solution)/shard_map/ppermute | solution.py:62
  157.2 10.4 %collective-permute-start.13 = (f32[128,256]{0,1:T(8,128)S(1)}, f32[128,256]{0,1:T(8,128)S(1)}, u32[]{:S(2)}, u32[]{:S(2)}) collective-permute-start(f32[128,256]{0,1:T(8,128)S(1)} %maximum_select_fusion.2), channel_id=1, source_target_pairs={{0,4},{4,0},{1,5},{5,1},{2,6},{6,2},{3,7},{7,3},{8,12},{12,8},{9,1... | collective-permute-start | bytes 393224 | tf_op jit(solution)/shard_map/ppermute | solution.py:62
  216.3 4.8 %collective-permute-start.14 = (f32[128,256]{1,0:T(8,128)S(1)}, f32[128,256]{1,0:T(8,128)S(1)}, u32[]{:S(2)}, u32[]{:S(2)}) collective-permute-start(f32[128,256]{1,0:T(8,128)S(1)} %get-tuple-element.74), channel_id=1, source_target_pairs={{0,8},{8,0},{16,24},{24,16},{32,40},{40,32},{48,56},{56,48},{64,72... | collective-permute-start | bytes 393224 | tf_op jit(solution)/shard_map/ppermute | solution.py:54
  221.1 8.6 %collective-permute-start.15 = (f32[128,256]{1,0:T(8,128)S(1)}, f32[128,256]{1,0:T(8,128)S(1)}, u32[]{:S(2)}, u32[]{:S(2)}) collective-permute-start(f32[128,256]{1,0:T(8,128)S(1)} %add.194), channel_id=1, source_target_pairs={{0,16},{8,24},{16,0},{24,8},{32,48},{40,56},{48,32},{56,40},{64,80... | collective-permute-start | bytes 393224 | tf_op jit(solution)/shard_map/ppermute | solution.py:54
  229.7 7.9 %collective-permute-start.16 = (f32[128,256]{1,0:T(8,128)S(1)}, f32[128,256]{1,0:T(8,128)S(1)}, u32[]{:S(2)}, u32[]{:S(2)}) collective-permute-start(f32[128,256]{1,0:T(8,128)S(1)} %add.195), channel_id=1, source_target_pairs={{0,32},{8,40},{16,48},{24,56},{32,0},{40,8},{48,16},{56,24},{64,96... | collective-permute-start | bytes 393224 | tf_op jit(solution)/shard_map/ppermute | solution.py:54
  237.7 25.9 %collective-permute-start.17 = (f32[128,256]{1,0:T(8,128)S(1)}, f32[128,256]{1,0:T(8,128)S(1)}, u32[]{:S(2)}, u32[]{:S(2)}) collective-permute-start(f32[128,256]{1,0:T(8,128)S(1)} %add.196), channel_id=1, source_target_pairs={{0,64},{8,72},{16,80},{24,88},{32,96},{40,104},{48,112},{56,120},{... | collective-permute-start | bytes 393224 | tf_op jit(solution)/shard_map/ppermute | solution.py:54
  263.6 5.4 %collective-permute-start.18 = (f32[128,256]{1,0:T(8,128)S(1)}, f32[128,256]{1,0:T(8,128)S(1)}, u32[]{:S(2)}, u32[]{:S(2)}) collective-permute-start(f32[128,256]{1,0:T(8,128)S(1)} %add.197), channel_id=1, source_target_pairs={{0,128},{8,136},{16,144},{24,152},{32,160},{40,168},{48,176},{56,1... | collective-permute-start | bytes 393224 | tf_op jit(solution)/shard_map/ppermute | solution.py:54
  273.0 5.6 %collective-permute-start.20 = (f32[128,256]{1,0:T(8,128)S(1)}, f32[128,256]{1,0:T(8,128)S(1)}, u32[]{:S(2)}, u32[]{:S(2)}) collective-permute-start(f32[128,256]{1,0:T(8,128)S(1)} %add.199), channel_id=1, source_target_pairs={{0,2},{1,3},{2,0},{3,1},{4,6},{5,7},{6,4},{7,5},{8,10},{9,11},{10,... | collective-permute-start | bytes 393224 | tf_op jit(solution)/shard_map/ppermute | solution.py:54
  279.7 20.5 %collective-permute-start.21 = (f32[256,256]{0,1:T(8,128)S(1)}, f32[256,256]{0,1:T(8,128)S(1)}, u32[]{:S(2)}, u32[]{:S(2)}) collective-permute-start(f32[256,256]{0,1:T(8,128)S(1)} %fusion.92), channel_id=1, source_target_pairs={{0,4},{4,0},{1,5},{5,1},{2,6},{6,2},{3,7},{7,3},{8,12},{12,8},{9,1... | collective-permute-start | bytes 786440 | tf_op jit(solution)/shard_map/ppermute | solution.py:54
  347.9 5.1 %collective-permute-start.22 = (f32[128,256]{1,0:T(8,128)S(1)}, f32[128,256]{1,0:T(8,128)S(1)}, u32[]{:S(2)}, u32[]{:S(2)}) collective-permute-start(f32[128,256]{1,0:T(8,128)S(1)} %get-tuple-element.77), channel_id=1, source_target_pairs={{0,8},{8,0},{16,24},{24,16},{32,40},{40,32},{48,56},{56,48},{64,72... | collective-permute-start | bytes 393224 | tf_op jit(solution)/shard_map/ppermute | solution.py:54
  353.0 8.5 %collective-permute-start.23 = (f32[128,256]{1,0:T(8,128)S(1)}, f32[128,256]{1,0:T(8,128)S(1)}, u32[]{:S(2)}, u32[]{:S(2)}) collective-permute-start(f32[128,256]{1,0:T(8,128)S(1)} %add.204), channel_id=1, source_target_pairs={{0,16},{8,24},{16,0},{24,8},{32,48},{40,56},{48,32},{56,40},{64,80... | collective-permute-start | bytes 393224 | tf_op jit(solution)/shard_map/ppermute | solution.py:54
  361.5 28.3 %collective-permute-start.24 = (f32[128,256]{1,0:T(8,128)S(1)}, f32[128,256]{1,0:T(8,128)S(1)}, u32[]{:S(2)}, u32[]{:S(2)}) collective-permute-start(f32[128,256]{1,0:T(8,128)S(1)} %add.205), channel_id=1, source_target_pairs={{0,32},{8,40},{16,48},{24,56},{32,0},{40,8},{48,16},{56,24},{64,96... | collective-permute-start | bytes 393224 | tf_op jit(solution)/shard_map/ppermute | solution.py:54
  393.8 5.4 %collective-permute-start.26 = (f32[128,256]{1,0:T(8,128)S(1)}, f32[128,256]{1,0:T(8,128)S(1)}, u32[]{:S(2)}, u32[]{:S(2)}) collective-permute-start(f32[128,256]{1,0:T(8,128)S(1)} %add.207), channel_id=1, source_target_pairs={{0,128},{8,136},{16,144},{24,152},{32,160},{40,168},{48,176},{56,1... | collective-permute-start | bytes 393224 | tf_op jit(solution)/shard_map/ppermute | solution.py:54
  399.3 4.8 %collective-permute-start.27 = (f32[128,256]{1,0:T(8,128)S(1)}, f32[128,256]{1,0:T(8,128)S(1)}, u32[]{:S(2)}, u32[]{:S(2)}) collective-permute-start(f32[128,256]{1,0:T(8,128)S(1)} %add.208), channel_id=1, source_target_pairs={{0,4},{4,0},{1,5},{5,1},{2,6},{6,2},{3,7},{7,3},{8,12},{12,8},{9,1... | collective-permute-start | bytes 393224 | tf_op jit(solution)/shard_map/ppermute | solution.py:54
  (11 other events, 174.0 us)
